TPU v7x, 128 devices: a whole 4x4x4 slice. The times are simulated.
128 devices in a mesh: expert: 64 (over x, z, y_hi, core), dp: 2 (over y_lo).
Axes of the slice: x: 4, y: 4 (y_hi: 2, y_lo: 2; y = y_hi * 2 + y_lo), z: 4, core: 2. Of those that a mesh axis runs over, the one named last changes fastest.
Arguments:
- tokens: bfloat16 [16384, 3584], P(('expert', 'dp')), may hold values from -6 to 6
- cotangent: bfloat16 [16384, 1024], P(('expert', 'dp')), may hold values from -4 to 4
- routing: int32 [16384, 1], P(('expert', 'dp')), may hold values from 0 to 63, as said below
- w_gate: bfloat16 [64, 3584, 1024], P('expert', None, 'dp'), may hold values from -0.09375 to 0.09375
- w_up: bfloat16 [64, 3584, 1024], P('expert', None, 'dp'), may hold values from -0.09375 to 0.09375
Outputs:
- grad_tokens: bfloat16 [16384, 3584], P(('expert', 'dp'))
- grad_gate: bfloat16 [64, 3584, 1024], P('expert', None, 'dp')
- grad_up: bfloat16 [64, 3584, 1024], P('expert', None, 'dp')
Inputs may be any that keep to these rules, and one draw needn't show every extreme that they name: `routing`: among the rows of one device no expert is named more than 4 times, and some device names some expert exactly 4 times. Of the experts e and e + 32, one is drawn busy and the other quiet.
All inputs are finite; a program needn't handle non-finite values.
Results may differ from a plain program's by a relative error of at most 0.005.
Values may be sent and summed in bfloat16 or wider, within the bound.
No kernel may reach another device: no remote copies, remote signals or barrier semaphores. Data moves between devices by JAX's collectives and lax.ppermute only.
A program may use at most 128 MiB of HBM per device.

v0:
```python
import jax
import jax.numpy as jnp
from jax import lax
from jax.sharding import PartitionSpec as P


def expert_math(rows, cot, weight_gate, weight_up):
    gate_act = jnp.dot(rows, weight_gate, preferred_element_type=jnp.float32)
    up_act = jnp.dot(rows, weight_up, preferred_element_type=jnp.float32)
    sigmoid_gate = jax.nn.sigmoid(gate_act)
    cot_float = cot.astype(jnp.float32)
    d_up = (cot_float * gate_act * sigmoid_gate).astype(jnp.bfloat16)
    d_gate = (
        cot_float * up_act * sigmoid_gate * (1.0 + gate_act * (1.0 - sigmoid_gate))
    ).astype(jnp.bfloat16)
    back = lax.dot_general(
        d_gate, weight_gate, (((1,), (1,)), ((), ())), preferred_element_type=jnp.float32
    )
    back = back + lax.dot_general(
        d_up, weight_up, (((1,), (1,)), ((), ())), preferred_element_type=jnp.float32
    )
    grad_g = lax.dot_general(
        rows, d_gate, (((0,), (0,)), ((), ())), preferred_element_type=jnp.float32
    )
    grad_u = lax.dot_general(
        rows, d_up, (((0,), (0,)), ((), ())), preferred_element_type=jnp.float32
    )
    return back.astype(jnp.bfloat16), grad_g.astype(jnp.bfloat16), grad_u.astype(jnp.bfloat16)


def per_device(tokens, cotangent, routing, w_gate, w_up):
    n_experts = lax.axis_size("expert")
    n_dp = lax.axis_size("dp")
    tok_rows, model_width = tokens.shape
    hidden = cotangent.shape[1]
    half_width = hidden // n_dp
    most_rows = max(2, tok_rows // 32, tok_rows // n_experts)
    slot_total = n_experts * most_rows

    expert_of = routing[:, 0]
    one_hot = (expert_of[:, None] == jnp.arange(n_experts, dtype=jnp.int32)[None, :]).astype(
        jnp.int32
    )
    slot_of = jnp.sum(jnp.cumsum(one_hot, axis=0) * one_hot, axis=1) - 1
    dest = expert_of * most_rows + slot_of
    pick = (jnp.arange(slot_total, dtype=jnp.int32)[:, None] == dest[None, :]).astype(
        jnp.bfloat16
    )
    send_rows = jnp.dot(pick, tokens, preferred_element_type=jnp.float32).astype(jnp.bfloat16)
    send_cot = jnp.dot(pick, cotangent, preferred_element_type=jnp.float32).astype(jnp.bfloat16)
    send_rows = send_rows.reshape(n_experts, 1, most_rows, model_width)
    send_cot = jnp.swapaxes(
        send_cot.reshape(n_experts, most_rows, n_dp, half_width), 1, 2
    )
    packed = jnp.concatenate(
        [
            jnp.broadcast_to(send_rows, (n_experts, n_dp, most_rows, model_width)),
            send_cot,
        ],
        axis=3,
    ).reshape(n_experts * n_dp * most_rows, model_width + half_width)
    got = lax.all_to_all(packed, ("expert", "dp"), split_axis=0, concat_axis=0, tiled=True)
    got_rows = got[:, :model_width]
    got_cot = got[:, model_width:]

    back, grad_g, grad_u = expert_math(got_rows, got_cot, w_gate[0], w_up[0])

    returned = lax.all_to_all(back, ("expert", "dp"), split_axis=0, concat_axis=0, tiled=True)
    returned = returned.reshape(n_experts, n_dp, most_rows, model_width).astype(jnp.float32)
    summed = jnp.sum(returned, axis=1).astype(jnp.bfloat16).reshape(slot_total, model_width)
    grad_tokens = lax.dot_general(
        pick, summed, (((0,), (0,)), ((), ())), preferred_element_type=jnp.float32
    ).astype(jnp.bfloat16)
    return grad_tokens, grad_g[None], grad_u[None]


def solution(mesh):
    placed = (
        P(("expert", "dp"), None),
        P(("expert", "dp"), None),
        P(("expert", "dp"), None),
        P("expert", None, "dp"),
        P("expert", None, "dp"),
    )
    return jax.shard_map(
        per_device,
        mesh=mesh,
        in_specs=placed,
        out_specs=(P(("expert", "dp"), None), P("expert", None, "dp"), P("expert", None, "dp")),
        check_vma=False,
    )
```

profile of v0, /device:TPU:1, one launch (start us, length us, event | category | flops | bytes accessed | tf_op | source)
XLA Modules:
  0.0 167.2 jit_solution(9271563800276837238)
XLA Ops:
  0.6 0.0 copy-start
  0.6 0.8 fusion.38
  1.5 0.2 reduce_window_sum.11
  1.6 0.8 select_reduce_fusion
  2.5 0.7 add_add_fusion
  3.1 1.2 convolution_convert_fusion.4
  4.4 0.4 reshape.33
  4.8 0.2 copy.8
  5.0 0.0 copy-done
  5.0 0.6 convolution_convert_fusion.2
  5.6 1.5 broadcast_in_dim.16
  7.1 2.4 %broadcast_in_dim.17 = bf16[64,2,4,3584]{3,2,1,0:T(4,128)(2,1)S(1)} broadcast(bf16[64,4,3584]{2,1,0:T(4,128)(2,1)} %broadcast_in_dim.16), dimensions={0,2,3} | broadcast | bytes 5505024 | tf_op jit(solution)/shard_map/broadcast_in_dim | solution.py:57
  9.5 2.6 %pad_maximum_fusion = bf16[64,2,4,4096]{3,2,1,0:T(4,128)(2,1)S(1)} fusion(bf16[64,2,4,512]{3,2,1,0:T(4,128)(2,1)S(1)} %copy.8, bf16[64,2,4,3584]{3,2,1,0:T(4,128)(2,1)S(1)} %broadcast_in_dim.17), kind=kLoop, calls=%fused_computation.7 | loop fusion | flops 8388608 | bytes 8388608 | tf_op jit(solution)/shard_map/concatenate | solution.py:55
  12.1 64.1 %all_to_all.21 = bf16[128,4,4096]{2,1,0:T(4,128)(2,1)} all-to-all(bf16[128,4,4096]{2,1,0:T(4,128)(2,1)S(1)} %bitcast.33), channel_id=1, replica_groups=mesh['expert'=64,'dp'=2] {'expert','dp'}, dimensions={0} | all-to-all | bytes 8388608 | tf_op jit(solution)/shard_map/all_to_all | solution.py:62
  76.2 6.9 %all_to_all.16 = bf16[512,4096]{1,0:T(8,128)(2,1)} reshape(bf16[128,4,4096]{2,1,0:T(4,128)(2,1)} %all_to_all.21) | data formatting | bytes 8388608 | tf_op jit(solution)/shard_map/all_to_all | solution.py:62
  83.2 0.0 copy-start.1
  83.2 0.0 copy-start.4
  83.2 5.3 %fusion.4 = f32[512,512]{1,0:T(8,128)S(1)} fusion(bf16[1,3584,512]{2,1,0:T(8,128)(2,1)} %param.8, bf16[512,4096]{1,0:T(8,128)(2,1)} %all_to_all.16), kind=kOutput, calls=%fused_computation.11 | convolution fusion | flops 1879048192 | bytes 8388608 | tf_op jit(solution)/shard_map/dot_general | solution.py:8
  88.5 0.0 copy-done.1
  88.5 0.1 copy-done.4
  88.6 0.0 copy-start.3
  88.6 2.3 %fusion.28 = bf16[512,512]{1,0:T(8,128)(2,1)S(1)} fusion(bf16[1,3584,512]{2,1,0:T(8,128)(2,1)S(1)} %copy-done.4, bf16[512,4096]{1,0:T(8,128)(2,1)S(1)} %copy-done.1, f32[512,512]{1,0:T(8,128)S(1)} %fusion.4), kind=kOutput, calls=%fused_computation.24 | convolution fusion | flops 1881931776 | bytes 9437184 | tf_op jit(solution)/shard_map/dot_general | solution.py:9
  90.9 0.0 copy-done.3
  90.9 2.1 %fusion.2 = f32[512,3584]{1,0:T(8,128)S(1)} fusion(bf16[512,512]{1,0:T(8,128)(2,1)S(1)} %fusion.28, bf16[1,3584,512]{2,1,0:T(8,128)(2,1)S(1)} %copy-done.3), kind=kOutput, calls=%fused_computation.9 | convolution fusion | flops 1879048192 | bytes 11534336 | tf_op jit(solution)/shard_map/dot_general | solution.py:16
  93.0 4.0 %add_convert_fusion = bf16[512,3584]{1,0:T(8,128)(2,1)} fusion(f32[512,3584]{1,0:T(8,128)S(1)} %fusion.2, bf16[1,3584,512]{2,1,0:T(8,128)(2,1)S(1)} %copy-done.4, f32[512,512]{1,0:T(8,128)S(1)} %fusion.4, bf16[512,4096]{1,0:T(8,128)(2,1)S(1)} %copy-done.1), kind=kOutput, calls=%fused_computation | convolution fusion | flops 1884553216 | bytes 16252928 | tf_op jit(solution)/shard_map/dot_general | solution.py:19
  97.0 7.0 %all_to_all.17 = bf16[128,4,3584]{2,1,0:T(4,128)(2,1)} reshape(bf16[512,3584]{1,0:T(8,128)(2,1)} %add_convert_fusion) | data formatting | bytes 7340032 | tf_op jit(solution)/shard_map/all_to_all | solution.py:68
  104.0 5.6 %all-to-all-start.1 = ((bf16[128,4,3584]{2,1,0:T(4,128)(2,1)}), bf16[128,4,3584]{2,1,0:T(4,128)(2,1)}, u32[]{:S(2)}, u32[]{:S(2)}) async-start(bf16[128,4,3584]{2,1,0:T(4,128)(2,1)} %all_to_all.17), calls=%async_computation.1 | async-start | bytes 7340032 | tf_op jit(solution)/shard_map/all_to_all | solution.py:68
  109.6 0.0 copy-start.2
  109.6 6.1 %fusion = bf16[1,3584,512]{2,1,0:T(8,128)(2,1)} fusion(bf16[512,512]{1,0:T(8,128)(2,1)S(1)} %fusion.28, bf16[512,4096]{1,0:T(8,128)(2,1)} %all_to_all.16), kind=kOutput, calls=%fused_computation.3 | convolution fusion | flops 1880883200 | bytes 7864320 | tf_op jit(solution)/shard_map/dot_general | solution.py:22
  115.7 0.0 copy-done.2
  115.7 4.1 %fusion.1 = bf16[1,3584,512]{2,1,0:T(8,128)(2,1)} fusion(bf16[512,4096]{1,0:T(8,128)(2,1)S(1)} %copy-done.2, f32[512,512]{1,0:T(8,128)S(1)} %fusion.4), kind=kOutput, calls=%fused_computation.4 | convolution fusion | flops 1882718208 | bytes 8912896 | tf_op jit(solution)/shard_map/dot_general | solution.py:25
  119.8 36.7 %all-to-all-done.1 = bf16[128,4,3584]{2,1,0:T(4,128)(2,1)} async-done(((bf16[128,4,3584]{2,1,0:T(4,128)(2,1)}), bf16[128,4,3584]{2,1,0:T(4,128)(2,1)}, u32[]{:S(2)}, u32[]{:S(2)}) %all-to-all-start.1) | async-done | bytes 3670048 | tf_op jit(solution)/shard_map/all_to_all | solution.py:68
  156.6 6.3 %bitcast_reduce_fusion = bf16[64,4,3584]{2,1,0:T(4,128)(2,1)} fusion(bf16[128,4,3584]{2,1,0:T(4,128)(2,1)} %all-to-all-done.1), kind=kLoop, calls=%fused_computation.8 | loop fusion | flops 917504 | bytes 5505024 | tf_op jit(solution)/shard_map/reduce_sum | solution.py:70
  162.9 2.9 %reshape.35 = bf16[256,3584]{1,0:T(8,128)(2,1)S(1)} reshape(bf16[64,4,3584]{2,1,0:T(4,128)(2,1)} %bitcast_reduce_fusion) | data formatting | bytes 3670016 | tf_op jit(solution)/shard_map/reshape | solution.py:70
  165.8 1.4 convolution_convert_fusion.3
Async XLA Ops:
  0.6 4.3 %copy-start = (bf16[128,3584]{1,0:T(8,128)(2,1)S(1)}, bf16[128,3584]{1,0:T(8,128)(2,1)}, u32[]{:S(2)}) copy-start(bf16[128,3584]{1,0:T(8,128)(2,1)} %param.5) | copy-start | bytes 2752516
  83.2 5.4 %copy-start.1 = (bf16[512,4096]{1,0:T(8,128)(2,1)S(1)}, bf16[512,4096]{1,0:T(8,128)(2,1)}, u32[]{:S(2)}) copy-start(bf16[512,4096]{1,0:T(8,128)(2,1)} %all_to_all.16) | copy-start | bytes 12582916
  83.2 5.5 %copy-start.4 = (bf16[1,3584,512]{2,1,0:T(8,128)(2,1)S(1)}, bf16[1,3584,512]{2,1,0:T(8,128)(2,1)}, u32[]{:S(2)}) copy-start(bf16[1,3584,512]{2,1,0:T(8,128)(2,1)} %param.9) | copy-start | bytes 11010052
  88.6 2.3 %copy-start.3 = (bf16[1,3584,512]{2,1,0:T(8,128)(2,1)S(1)}, bf16[1,3584,512]{2,1,0:T(8,128)(2,1)}, u32[]{:S(2)}) copy-start(bf16[1,3584,512]{2,1,0:T(8,128)(2,1)} %param.8) | copy-start | bytes 11010052
  104.0 52.6 %all-to-all-start.1 = ((bf16[128,4,3584]{2,1,0:T(4,128)(2,1)}), bf16[128,4,3584]{2,1,0:T(4,128)(2,1)}, u32[]{:S(2)}, u32[]{:S(2)}) async-start(bf16[128,4,3584]{2,1,0:T(4,128)(2,1)} %all_to_all.17), calls=%async_computation.1 | async-start | bytes 7340032 | tf_op jit(solution)/shard_map/all_to_all | solution.py:68
  109.6 6.1 %copy-start.2 = (bf16[512,4096]{1,0:T(8,128)(2,1)S(1)}, bf16[512,4096]{1,0:T(8,128)(2,1)}, u32[]{:S(2)}) copy-start(bf16[512,4096]{1,0:T(8,128)(2,1)} %all_to_all.16) | copy-start | bytes 12582916
where the time goes:
time: 168 us; the launch traced here: 167 us
  blocking collectives  64.1 us (38%)
  waiting for transfers between devices  36.7 us (22%)
  matrix products  27.1 us (16%)
  local copies, waits for them, and re-layouts  21.4 us (13%)
  other arithmetic  11.4 us (7%)
  starting transfers between devices  5.61 us (3%)
    all_to_all x1, blocking collectives, per_device(): lax.all_to_all(packed, ('expert', 'dp'), split_axis=0, concat_axis=0, til...  64.1 us
    all_to_all x1, waiting for transfers between devices, per_device(): lax.all_to_all(back, ('expert', 'dp'), split_axis=0, concat_axis=0, tiled...  36.7 us
    all_to_all x1, local copies, waits for them, and re-layouts, per_device(): lax.all_to_all(back, ('expert', 'dp'), split_axis=0, concat_axis=0, tiled...  6.99 us
    all_to_all x1, local copies, waits for them, and re-layouts, per_device(): lax.all_to_all(packed, ('expert', 'dp'), split_axis=0, concat_axis=0, til...  6.92 us
    reduce_sum x1, other arithmetic, per_device(): jnp.sum(returned, axis=1).astype(jnp.bfloat16)  6.32 us
    dot_general x1, matrix products, expert_math(): lax.dot_general(rows, d_gate, (((0,), (0,)), ((), ())), preferred_element...  6.13 us
    all_to_all x1, starting transfers between devices, per_device(): lax.all_to_all(back, ('expert', 'dp'), split_axis=0, concat_axis=0, tiled...  5.61 us
    dot_general x1, matrix products, expert_math(): gate_act = jnp.dot(rows, weight_gate, preferred_element_type=jnp.float32)  5.34 us
  transfers between devices with their start and end apart: 1, of which 1 were waited for; matrix products, arithmetic and copies ran while one was open for 6% of the time, Pallas kernels for 0%

commit v1 on v0

--- a/solution.py
+++ b/solution.py
@@ -5,26 +5,18 @@
 
 
 def expert_math(rows, cot, weight_gate, weight_up):
-    gate_act = jnp.dot(rows, weight_gate, preferred_element_type=jnp.float32)
-    up_act = jnp.dot(rows, weight_up, preferred_element_type=jnp.float32)
+    gate_act = jnp.einsum("skd,df->skf", rows, weight_gate, preferred_element_type=jnp.float32)
+    up_act = jnp.einsum("skd,df->skf", rows, weight_up, preferred_element_type=jnp.float32)
     sigmoid_gate = jax.nn.sigmoid(gate_act)
     cot_float = cot.astype(jnp.float32)
     d_up = (cot_float * gate_act * sigmoid_gate).astype(jnp.bfloat16)
     d_gate = (
         cot_float * up_act * sigmoid_gate * (1.0 + gate_act * (1.0 - sigmoid_gate))
     ).astype(jnp.bfloat16)
-    back = lax.dot_general(
-        d_gate, weight_gate, (((1,), (1,)), ((), ())), preferred_element_type=jnp.float32
-    )
-    back = back + lax.dot_general(
-        d_up, weight_up, (((1,), (1,)), ((), ())), preferred_element_type=jnp.float32
-    )
-    grad_g = lax.dot_general(
-        rows, d_gate, (((0,), (0,)), ((), ())), preferred_element_type=jnp.float32
-    )
-    grad_u = lax.dot_general(
-        rows, d_up, (((0,), (0,)), ((), ())), preferred_element_type=jnp.float32
-    )
+    back = jnp.einsum("skf,df->skd", d_gate, weight_gate, preferred_element_type=jnp.float32)
+    back = back + jnp.einsum("skf,df->skd", d_up, weight_up, preferred_element_type=jnp.float32)
+    grad_g = jnp.einsum("skd,skf->df", rows, d_gate, preferred_element_type=jnp.float32)
+    grad_u = jnp.einsum("skd,skf->df", rows, d_up, preferred_element_type=jnp.float32)
     return back.astype(jnp.bfloat16), grad_g.astype(jnp.bfloat16), grad_u.astype(jnp.bfloat16)
 
 
@@ -59,17 +51,19 @@
         ],
         axis=3,
     ).reshape(n_experts * n_dp * most_rows, model_width + half_width)
+    packed = packed.reshape(n_experts * n_dp, most_rows, model_width + half_width)
     got = lax.all_to_all(packed, ("expert", "dp"), split_axis=0, concat_axis=0, tiled=True)
-    got_rows = got[:, :model_width]
-    got_cot = got[:, model_width:]
+    got_rows = got[:, :, :model_width]
+    got_cot = got[:, :, model_width:]
 
     back, grad_g, grad_u = expert_math(got_rows, got_cot, w_gate[0], w_up[0])
 
     returned = lax.all_to_all(back, ("expert", "dp"), split_axis=0, concat_axis=0, tiled=True)
-    returned = returned.reshape(n_experts, n_dp, most_rows, model_width).astype(jnp.float32)
-    summed = jnp.sum(returned, axis=1).astype(jnp.bfloat16).reshape(slot_total, model_width)
+    pick_dup = jnp.broadcast_to(
+        pick.reshape(n_experts, 1, most_rows, tok_rows), (n_experts, n_dp, most_rows, tok_rows)
+    ).reshape(n_experts * n_dp, most_rows, tok_rows)
     grad_tokens = lax.dot_general(
-        pick, summed, (((0,), (0,)), ((), ())), preferred_element_type=jnp.float32
+        pick_dup, returned, (((0, 1), (0, 1)), ((), ())), preferred_element_type=jnp.float32
     ).astype(jnp.bfloat16)
     return grad_tokens, grad_g[None], grad_u[None]
 

time: 168 us -> 150 us (0.89)
  local copies, waits for them, and re-layouts: 21.4 us -> 12.5 us
  other arithmetic: 11.4 us -> 5.18 us
  matrix products: 27.1 us -> 24.5 us
    all_to_all x2 -> x0, local copies, waits for them, and re-layouts: 13.9 us -> none  [the longest x1 6.99 us: per_device(): lax.all_to_all(back, ('expert', 'dp'), split_axis=0, concat_axis=0, tiled...]
    reduce_sum x1 -> x0, other arithmetic: 6.32 us -> none  [per_device(): jnp.sum(returned, axis=1).astype(jnp.bfloat16)]
    convert_element_type x0 -> x1, local copies, waits for them, and re-layouts: none -> 4.67 us  [expert_math(): back.astype(jnp.bfloat16)]
    reshape x1 -> x0, local copies, waits for them, and re-layouts: 2.94 us -> none  [per_device(): jnp.sum(returned, axis=1).astype(jnp.bfloat16)]
    dot_general x7, matrix products: 25.3 us -> 22.7 us  [the longest x1 6.14 us: expert_math(): jnp.einsum('skd,skf->df', rows, d_gate, preferred_element_type=jnp.float32)]
    slice x0 -> x2, local copies, waits for them, and re-layouts: none -> 2.07 us  [the longest x1 1.81 us: per_device(): got_rows = got[:, :, :model_width]]
  transfers between devices with their start and end apart: 1 -> 1, of which waited for: 1 -> 1; matrix products, arithmetic and copies ran while one was open for 6% -> 7% of each run, Pallas kernels for 0% -> 0%
where the time goes in v1:
time: 150 us
  blocking collectives  64 us (43%)
  waiting for transfers between devices  36.6 us (24%)
  matrix products  24.5 us (16%)
  local copies, waits for them, and re-layouts  12.5 us (8%)
  starting transfers between devices  5.82 us (4%)
  other arithmetic  5.18 us (3%)
    all_to_all x1, blocking collectives, per_device(): lax.all_to_all(packed, ('expert', 'dp'), split_axis=0, concat_axis=0, til...  64 us
    all_to_all x1, waiting for transfers between devices, per_device(): lax.all_to_all(back, ('expert', 'dp'), split_axis=0, concat_axis=0, tiled...  36.6 us
    dot_general x1, matrix products, expert_math(): jnp.einsum('skd,skf->df', rows, d_gate, preferred_element_type=jnp.float32)  6.14 us
    all_to_all x1, starting transfers between devices, per_device(): lax.all_to_all(back, ('expert', 'dp'), split_axis=0, concat_axis=0, tiled...  5.82 us
    convert_element_type x1, local copies, waits for them, and re-layouts, expert_math(): back.astype(jnp.bfloat16)  4.67 us
    dot_general x1, matrix products, expert_math(): jnp.einsum('skd,skf->df', rows, d_up, preferred_element_type=jnp.float32)  4.07 us
    broadcast_in_dim x2, local copies, waits for them, and re-layouts, per_device(): jnp.broadcast_to(send_rows, (n_experts, n_dp, most_rows, model_width))  3.9 us
    dot_general x1, matrix products, per_device(): lax.dot_general(pick_dup, returned, (((0, 1), (0, 1)), ((), ())), preferr...  3.89 us
  transfers between devices with their start and end apart: 1, of which 1 were waited for; matrix products, arithmetic and copies ran while one was open for 7% of the time, Pallas kernels for 0%

profile of v1, /device:TPU:1, one launch (start us, length us, event | category | flops | bytes accessed | tf_op | source)
XLA Modules:
  0.0 149.5 jit_solution(15532801690865264892)
XLA Ops:
  0.6 0.0 copy-start
  0.6 0.8 fusion.39
  1.5 0.2 reduce_window_sum.11
  1.6 0.8 select_reduce_fusion
  2.5 0.7 add_add_fusion
  3.1 1.2 convolution_convert_fusion.1
  4.4 0.4 reshape.43
  4.8 0.2 copy.17
  5.0 0.0 copy-done
  5.0 0.6 convolution_convert_fusion
  5.6 1.5 broadcast_in_dim.22
  7.1 2.4 %broadcast_in_dim.23 = bf16[64,2,4,3584]{3,2,1,0:T(4,128)(2,1)S(1)} broadcast(bf16[64,4,3584]{2,1,0:T(4,128)(2,1)} %broadcast_in_dim.22), dimensions={0,2,3} | broadcast | bytes 5505024 | tf_op jit(solution)/shard_map/broadcast_in_dim | solution.py:49
  9.5 2.6 %pad_maximum_fusion = bf16[64,2,4,4096]{3,2,1,0:T(4,128)(2,1)S(1)} fusion(bf16[64,2,4,512]{3,2,1,0:T(4,128)(2,1)S(1)} %copy.17, bf16[64,2,4,3584]{3,2,1,0:T(4,128)(2,1)S(1)} %broadcast_in_dim.23), kind=kLoop, calls=%fused_computation.8 | loop fusion | flops 8388608 | bytes 8388608 | tf_op jit(solution)/shard_map/concatenate | solution.py:47
  12.1 64.0 %all_to_all.10 = bf16[128,4,4096]{2,1,0:T(4,128)(2,1)S(1)} all-to-all(bf16[128,4,4096]{2,1,0:T(4,128)(2,1)S(1)} %bitcast.46), channel_id=1, replica_groups=mesh['expert'=64,'dp'=2] {'expert','dp'}, dimensions={0} | all-to-all | bytes 8388608 | tf_op jit(solution)/shard_map/all_to_all | solution.py:55
  76.1 0.0 copy-start.3
  76.1 1.8 %slice.9 = bf16[128,4,3584]{2,1,0:T(4,128)(2,1)S(1)} slice(bf16[128,4,4096]{2,1,0:T(4,128)(2,1)S(1)} %all_to_all.10), slice={[0:128], [0:4], [0:3584]} | slice | bytes 7340032 | tf_op jit(solution)/shard_map/slice | solution.py:56
  77.9 0.2 copy-done.3
  78.2 0.0 copy-start.1
  78.2 0.0 copy-start.4
  78.2 2.1 %fusion.5 = f32[128,4,512]{2,0,1:T(8,128)S(1)} fusion(bf16[1,3584,512]{2,1,0:T(8,128)(2,1)S(1)} %copy-done.3, bf16[128,4,3584]{2,1,0:T(4,128)(2,1)S(1)} %slice.9), kind=kOutput, calls=%fused_computation.11 | convolution fusion | flops 1879048192 | bytes 8388608 | tf_op jit(solution)/shard_map/skd,df->skf/dot_general | solution.py:8
  80.2 0.3 slice.8
  80.5 0.0 copy-done.1
  80.5 1.0 copy-done.4
  81.5 2.3 %fusion.30 = bf16[128,4,512]{2,0,1:T(8,128)(2,1)S(1)} fusion(bf16[1,3584,512]{2,1,0:T(8,128)(2,1)S(1)} %copy-done.4, bf16[128,4,3584]{2,1,0:T(4,128)(2,1)S(1)} %slice.9, f32[128,4,512]{2,0,1:T(8,128)S(1)} %fusion.5, bf16[128,4,512]{2,1,0:T(4,128)(2,1)S(1)} %slice.8), kind=kOutput, calls=%fused_computation.25 | convolution fusion | flops 1881931776 | bytes 9437184 | tf_op jit(solution)/shard_map/skd,df->skf/dot_general | solution.py:9
  83.8 2.1 %fusion.3 = f32[128,4,3584]{2,0,1:T(8,128)S(1)} fusion(bf16[128,4,512]{2,0,1:T(8,128)(2,1)S(1)} %fusion.30, bf16[1,3584,512]{2,1,0:T(8,128)(2,1)S(1)} %copy-done.3), kind=kOutput, calls=%fused_computation.9 | convolution fusion | flops 1879048192 | bytes 11534336 | tf_op jit(solution)/shard_map/skf,df->skd/dot_general | solution.py:16
  86.0 2.1 %add_convert_fusion = bf16[128,4,3584]{2,0,1:T(8,128)(2,1)S(1)} fusion(f32[128,4,3584]{2,0,1:T(8,128)S(1)} %fusion.3, bf16[1,3584,512]{2,1,0:T(8,128)(2,1)S(1)} %copy-done.4, f32[128,4,512]{2,0,1:T(8,128)S(1)} %fusion.5, bf16[128,4,512]{2,1,0:T(4,128)(2,1)S(1)} %slice.8), kind=kOutput, calls=%fused_computation.2 | convolution fusion | flops 1884553216 | bytes 16252928 | tf_op jit(solution)/shard_map/skf,df->skd/dot_general | solution.py:17
  88.1 4.7 %copy.20 = bf16[128,4,3584]{2,1,0:T(4,128)(2,1)} copy(bf16[128,4,3584]{2,0,1:T(8,128)(2,1)S(1)} %add_convert_fusion) | data formatting | bytes 7340032 | tf_op jit(solution)/shard_map/convert_element_type | solution.py:20
  92.8 5.8 %all-to-all-start.1 = ((bf16[128,4,3584]{2,1,0:T(4,128)(2,1)}), bf16[128,4,3584]{2,1,0:T(4,128)(2,1)}, u32[]{:S(2)}, u32[]{:S(2)}) async-start(bf16[128,4,3584]{2,1,0:T(4,128)(2,1)} %copy.20), calls=%async_computation.1 | async-start | bytes 7340032 | tf_op jit(solution)/shard_map/all_to_all | solution.py:61
  98.6 0.1 compare_convert_fusion
  98.7 0.0 copy-start.2
  98.7 6.1 %fusion = bf16[1,3584,512]{2,1,0:T(8,128)(2,1)} fusion(bf16[128,4,512]{2,0,1:T(8,128)(2,1)S(1)} %fusion.30, bf16[128,4,3584]{2,1,0:T(4,128)(2,1)} %copy-done.1), kind=kOutput, calls=%fused_computation.3 | convolution fusion | flops 1880883200 | bytes 7864320 | tf_op jit(solution)/shard_map/skd,skf->df/dot_general | solution.py:18
  104.9 0.0 copy-done.2
  104.9 4.1 %fusion.1 = bf16[1,3584,512]{2,1,0:T(8,128)(2,1)} fusion(bf16[128,4,3584]{2,1,0:T(4,128)(2,1)S(1)} %copy-done.2, f32[128,4,512]{2,0,1:T(8,128)S(1)} %fusion.5, bf16[128,4,512]{2,1,0:T(4,128)(2,1)S(1)} %slice.8), kind=kOutput, calls=%fused_computation.4 | convolution fusion | flops 1882718208 | bytes 8912896 | tf_op jit(solution)/shard_map/skd,skf->df/dot_general | solution.py:19
  108.9 36.6 %all-to-all-done.1 = bf16[128,4,3584]{2,1,0:T(4,128)(2,1)} async-done(((bf16[128,4,3584]{2,1,0:T(4,128)(2,1)}), bf16[128,4,3584]{2,1,0:T(4,128)(2,1)}, u32[]{:S(2)}, u32[]{:S(2)}) %all-to-all-start.1) | async-done | bytes 3670048 | tf_op jit(solution)/shard_map/all_to_all | solution.py:61
  145.6 0.1 broadcast_in_dim.10
  145.7 3.9 %fusion.2 = bf16[128,3584]{1,0:T(8,128)(2,1)} fusion(bf16[128,4,128]{2,0,1:T(8,128)(2,1)S(1)} %bitcast.48, bf16[128,4,3584]{2,1,0:T(4,128)(2,1)} %all-to-all-done.1), kind=kOutput, calls=%fused_computation.7 | convolution fusion | flops 470220800 | bytes 4718592 | tf_op jit(solution)/shard_map/dot_general | solution.py:65
  (1 shorter events, 0.0 us)
Async XLA Ops:
  0.6 4.3 %copy-start = (bf16[128,3584]{1,0:T(8,128)(2,1)S(1)}, bf16[128,3584]{1,0:T(8,128)(2,1)}, u32[]{:S(2)}) copy-start(bf16[128,3584]{1,0:T(8,128)(2,1)} %param.5) | copy-start | bytes 2752516
  76.1 2.0 %copy-start.3 = (bf16[1,3584,512]{2,1,0:T(8,128)(2,1)S(1)}, bf16[1,3584,512]{2,1,0:T(8,128)(2,1)}, u32[]{:S(2)}) copy-start(bf16[1,3584,512]{2,1,0:T(8,128)(2,1)} %param.8) | copy-start | bytes 11010052
  78.2 2.4 %copy-start.1 = (bf16[128,4,3584]{2,1,0:T(4,128)(2,1)}, bf16[128,4,3584]{2,1,0:T(4,128)(2,1)S(1)}, u32[]{:S(2)}) copy-start(bf16[128,4,3584]{2,1,0:T(4,128)(2,1)S(1)} %slice.9) | copy-start | bytes 11010052
  78.2 3.4 %copy-start.4 = (bf16[1,3584,512]{2,1,0:T(8,128)(2,1)S(1)}, bf16[1,3584,512]{2,1,0:T(8,128)(2,1)}, u32[]{:S(2)}) copy-start(bf16[1,3584,512]{2,1,0:T(8,128)(2,1)} %param.9) | copy-start | bytes 11010052
  92.8 52.8 %all-to-all-start.1 = ((bf16[128,4,3584]{2,1,0:T(4,128)(2,1)}), bf16[128,4,3584]{2,1,0:T(4,128)(2,1)}, u32[]{:S(2)}, u32[]{:S(2)}) async-start(bf16[128,4,3584]{2,1,0:T(4,128)(2,1)} %copy.20), calls=%async_computation.1 | async-start | bytes 7340032 | tf_op jit(solution)/shard_map/all_to_all | solution.py:61
  98.7 6.2 %copy-start.2 = (bf16[128,4,3584]{2,1,0:T(4,128)(2,1)S(1)}, bf16[128,4,3584]{2,1,0:T(4,128)(2,1)}, u32[]{:S(2)}) copy-start(bf16[128,4,3584]{2,1,0:T(4,128)(2,1)} %copy-done.1) | copy-start | bytes 11010052

commit v2 on v1

--- a/solution.py
+++ b/solution.py
@@ -13,8 +13,12 @@
     d_gate = (
         cot_float * up_act * sigmoid_gate * (1.0 + gate_act * (1.0 - sigmoid_gate))
     ).astype(jnp.bfloat16)
-    back = jnp.einsum("skf,df->skd", d_gate, weight_gate, preferred_element_type=jnp.float32)
-    back = back + jnp.einsum("skf,df->skd", d_up, weight_up, preferred_element_type=jnp.float32)
+    back = jnp.einsum(
+        "skf,df->skd",
+        jnp.concatenate([d_gate, d_up], axis=2),
+        jnp.concatenate([weight_gate, weight_up], axis=1),
+        preferred_element_type=jnp.float32,
+    )
     grad_g = jnp.einsum("skd,skf->df", rows, d_gate, preferred_element_type=jnp.float32)
     grad_u = jnp.einsum("skd,skf->df", rows, d_up, preferred_element_type=jnp.float32)
     return back.astype(jnp.bfloat16), grad_g.astype(jnp.bfloat16), grad_u.astype(jnp.bfloat16)

time: 150 us -> 150 us (level)
    dot_general x2 -> x1, matrix products: 4.22 us -> 4.25 us  [expert_math(): jnp.einsum('skf,df->skd', jnp.concatenate([d_gate, d_up], axis=2), jnp.co...]
where the time goes in v2:
time: 150 us
  blocking collectives  64 us (43%)
  waiting for transfers between devices  36.8 us (25%)
  matrix products  24.6 us (16%)
  local copies, waits for them, and re-layouts  12.6 us (8%)
  starting transfers between devices  5.62 us (4%)
  other arithmetic  5.18 us (3%)
    all_to_all x1, blocking collectives, per_device(): lax.all_to_all(packed, ('expert', 'dp'), split_axis=0, concat_axis=0, til...  64 us
    all_to_all x1, waiting for transfers between devices, per_device(): lax.all_to_all(back, ('expert', 'dp'), split_axis=0, concat_axis=0, tiled...  36.8 us
    dot_general x1, matrix products, expert_math(): jnp.einsum('skd,skf->df', rows, d_gate, preferred_element_type=jnp.float32)  6.14 us
    all_to_all x1, starting transfers between devices, per_device(): lax.all_to_all(back, ('expert', 'dp'), split_axis=0, concat_axis=0, tiled...  5.62 us
    convert_element_type x1, local copies, waits for them, and re-layouts, expert_math(): back.astype(jnp.bfloat16)  4.67 us
    dot_general x1, matrix products, expert_math(): jnp.einsum('skf,df->skd', jnp.concatenate([d_gate, d_up], axis=2), jnp.co...  4.25 us
    dot_general x1, matrix products, expert_math(): jnp.einsum('skd,skf->df', rows, d_up, preferred_element_type=jnp.float32)  3.95 us
    broadcast_in_dim x2, local copies, waits for them, and re-layouts, per_device(): jnp.broadcast_to(send_rows, (n_experts, n_dp, most_rows, model_width))  3.9 us
  transfers between devices with their start and end apart: 1, of which 1 were waited for; matrix products, arithmetic and copies ran while one was open for 7% of the time, Pallas kernels for 0%

profile of v2, /device:TPU:1, one launch (start us, length us, event | category | flops | bytes accessed | tf_op | source)
XLA Modules:
  0.0 149.6 jit_solution(12726715862377370855)
XLA Ops:
  0.6 0.0 copy-start
  0.6 0.8 fusion.43
  1.5 0.2 reduce_window_sum.11
  1.6 0.8 select_reduce_fusion
  2.5 0.7 add_add_fusion
  3.1 1.2 convolution_convert_fusion.1
  4.4 0.4 reshape.43
  4.8 0.2 copy.17
  5.0 0.0 copy-done
  5.0 0.6 convolution_convert_fusion
  5.6 1.5 broadcast_in_dim.22
  7.1 2.4 %broadcast_in_dim.23 = bf16[64,2,4,3584]{3,2,1,0:T(4,128)(2,1)S(1)} broadcast(bf16[64,4,3584]{2,1,0:T(4,128)(2,1)} %broadcast_in_dim.22), dimensions={0,2,3} | broadcast | bytes 5505024 | tf_op jit(solution)/shard_map/broadcast_in_dim | solution.py:53
  9.5 2.6 %pad_maximum_fusion = bf16[64,2,4,4096]{3,2,1,0:T(4,128)(2,1)S(1)} fusion(bf16[64,2,4,512]{3,2,1,0:T(4,128)(2,1)S(1)} %copy.17, bf16[64,2,4,3584]{3,2,1,0:T(4,128)(2,1)S(1)} %broadcast_in_dim.23), kind=kLoop, calls=%fused_computation.12 | loop fusion | flops 8388608 | bytes 8388608 | tf_op jit(solution)/shard_map/concatenate | solution.py:51
  12.1 64.0 %all_to_all.10 = bf16[128,4,4096]{2,1,0:T(4,128)(2,1)S(1)} all-to-all(bf16[128,4,4096]{2,1,0:T(4,128)(2,1)S(1)} %bitcast.49), channel_id=1, replica_groups=mesh['expert'=64,'dp'=2] {'expert','dp'}, dimensions={0} | all-to-all | bytes 8388608 | tf_op jit(solution)/shard_map/all_to_all | solution.py:59
  76.1 0.3 slice.8
  76.4 0.0 copy-start.4
  76.4 1.8 %slice.9 = bf16[128,4,3584]{2,1,0:T(4,128)(2,1)S(1)} slice(bf16[128,4,4096]{2,1,0:T(4,128)(2,1)S(1)} %all_to_all.10), slice={[0:128], [0:4], [0:3584]} | slice | bytes 7340032 | tf_op jit(solution)/shard_map/slice | solution.py:60
  78.2 0.2 copy-done.4
  78.4 0.0 copy-start.1
  78.4 0.0 copy-start.3
  78.5 2.2 %fusion.37 = (bf16[128,4,512]{2,0,1:T(8,128)(2,1)S(1)}, f32[128,4,512]{2,0,1:T(8,128)S(1)}) fusion(bf16[128,4,512]{2,1,0:T(4,128)(2,1)S(1)} %slice.8, bf16[1,3584,512]{2,1,0:T(8,128)(2,1)S(1)} %copy-done.4, bf16[128,4,3584]{2,1,0:T(4,128)(2,1)S(1)} %slice.9), kind=kOutput, calls=%fused_computation.29 | convolution fusion | flops 1880883200 | bytes 9437184 | tf_op jit(solution)/shard_map/skd,df->skf/dot_general | solution.py:8
  80.7 0.0 copy-done.1
  80.7 1.1 copy-done.3
  81.8 2.3 %fusion.31 = bf16[128,4,512]{2,0,1:T(8,128)(2,1)S(1)} fusion(bf16[1,3584,512]{2,1,0:T(8,128)(2,1)S(1)} %copy-done.3, bf16[128,4,3584]{2,1,0:T(4,128)(2,1)S(1)} %slice.9, f32[128,4,512]{2,0,1:T(8,128)S(1)} %get-tuple-element.4, bf16[128,4,512]{2,1,0:T(4,128)(2,1)S(1)} %slice.8), kind=kOutput, calls=%fused_computation.26 | convolution fusion | flops 1881931776 | bytes 9437184 | tf_op jit(solution)/shard_map/skd,df->skf/dot_general | solution.py:9
  84.1 4.3 %fusion.3 = bf16[128,4,3584]{2,0,1:T(8,128)(2,1)S(1)} fusion(bf16[3584,512]{1,0:T(8,128)(2,1)S(1)} %bitcast.54, bf16[3584,512]{1,0:T(8,128)(2,1)S(1)} %bitcast.55, bf16[128,4,512]{2,0,1:T(8,128)(2,1)S(1)} %get-tuple-element.3, bf16[128,4,512]{2,0,1:T(8,128)(2,1)S(1)} %fusion.31), kind=kOutput, calls=%fused_computation.6 | convolution fusion | flops 3776708608 | bytes 12058624 | tf_op jit(solution)/shard_map/skf,df->skd/dot_general | solution.py:16
  88.4 4.7 %copy.20 = bf16[128,4,3584]{2,1,0:T(4,128)(2,1)} copy(bf16[128,4,3584]{2,0,1:T(8,128)(2,1)S(1)} %fusion.3) | data formatting | bytes 7340032 | tf_op jit(solution)/shard_map/convert_element_type | solution.py:24
  93.1 5.6 %all-to-all-start.1 = ((bf16[128,4,3584]{2,1,0:T(4,128)(2,1)}), bf16[128,4,3584]{2,1,0:T(4,128)(2,1)}, u32[]{:S(2)}, u32[]{:S(2)}) async-start(bf16[128,4,3584]{2,1,0:T(4,128)(2,1)} %copy.20), calls=%async_computation.1 | async-start | bytes 7340032 | tf_op jit(solution)/shard_map/all_to_all | solution.py:65
  98.7 0.1 compare_convert_fusion
  98.8 0.0 copy-start.2
  98.8 6.1 %fusion.4 = bf16[1,3584,512]{2,1,0:T(8,128)(2,1)} fusion(bf16[128,4,512]{2,0,1:T(8,128)(2,1)S(1)} %fusion.31, bf16[128,4,3584]{2,1,0:T(4,128)(2,1)} %copy-done.1), kind=kOutput, calls=%fused_computation.7 | convolution fusion | flops 1880883200 | bytes 7864320 | tf_op jit(solution)/shard_map/skd,skf->df/dot_general | solution.py:22
  105.0 0.0 copy-done.2
  105.0 3.9 %fusion.5 = bf16[1,3584,512]{2,1,0:T(8,128)(2,1)} fusion(bf16[128,4,512]{2,0,1:T(8,128)(2,1)S(1)} %get-tuple-element.3, bf16[128,4,3584]{2,1,0:T(4,128)(2,1)S(1)} %copy-done.2), kind=kOutput, calls=%fused_computation.8 | convolution fusion | flops 1880883200 | bytes 7864320 | tf_op jit(solution)/shard_map/skd,skf->df/dot_general | solution.py:23
  108.9 36.8 %all-to-all-done.1 = bf16[128,4,3584]{2,1,0:T(4,128)(2,1)} async-done(((bf16[128,4,3584]{2,1,0:T(4,128)(2,1)}), bf16[128,4,3584]{2,1,0:T(4,128)(2,1)}, u32[]{:S(2)}, u32[]{:S(2)}) %all-to-all-start.1) | async-done | bytes 3670048 | tf_op jit(solution)/shard_map/all_to_all | solution.py:65
  145.7 0.1 broadcast_in_dim.10
  145.7 3.9 %fusion.6 = bf16[128,3584]{1,0:T(8,128)(2,1)} fusion(bf16[128,4,128]{2,0,1:T(8,128)(2,1)S(1)} %bitcast.51, bf16[128,4,3584]{2,1,0:T(4,128)(2,1)} %all-to-all-done.1), kind=kOutput, calls=%fused_computation.11 | convolution fusion | flops 470220800 | bytes 4718592 | tf_op jit(solution)/shard_map/dot_general | solution.py:69
  (1 shorter events, 0.0 us)
Async XLA Ops:
  0.6 4.3 %copy-start = (bf16[128,3584]{1,0:T(8,128)(2,1)S(1)}, bf16[128,3584]{1,0:T(8,128)(2,1)}, u32[]{:S(2)}) copy-start(bf16[128,3584]{1,0:T(8,128)(2,1)} %param.5) | copy-start | bytes 2752516
  76.4 2.0 %copy-start.4 = (bf16[1,3584,512]{2,1,0:T(8,128)(2,1)S(1)}, bf16[1,3584,512]{2,1,0:T(8,128)(2,1)}, u32[]{:S(2)}) copy-start(bf16[1,3584,512]{2,1,0:T(8,128)(2,1)} %param.8) | copy-start | bytes 11010052
  78.4 2.2 %copy-start.1 = (bf16[128,4,3584]{2,1,0:T(4,128)(2,1)}, bf16[128,4,3584]{2,1,0:T(4,128)(2,1)S(1)}, u32[]{:S(2)}) copy-start(bf16[128,4,3584]{2,1,0:T(4,128)(2,1)S(1)} %slice.9) | copy-start | bytes 11010052
  78.4 3.4 %copy-start.3 = (bf16[1,3584,512]{2,1,0:T(8,128)(2,1)S(1)}, bf16[1,3584,512]{2,1,0:T(8,128)(2,1)}, u32[]{:S(2)}) copy-start(bf16[1,3584,512]{2,1,0:T(8,128)(2,1)} %param.9) | copy-start | bytes 11010052
  93.1 52.6 %all-to-all-start.1 = ((bf16[128,4,3584]{2,1,0:T(4,128)(2,1)}), bf16[128,4,3584]{2,1,0:T(4,128)(2,1)}, u32[]{:S(2)}, u32[]{:S(2)}) async-start(bf16[128,4,3584]{2,1,0:T(4,128)(2,1)} %copy.20), calls=%async_computation.1 | async-start | bytes 7340032 | tf_op jit(solution)/shard_map/all_to_all | solution.py:65
  98.8 6.2 %copy-start.2 = (bf16[128,4,3584]{2,1,0:T(4,128)(2,1)S(1)}, bf16[128,4,3584]{2,1,0:T(4,128)(2,1)}, u32[]{:S(2)}) copy-start(bf16[128,4,3584]{2,1,0:T(4,128)(2,1)} %copy-done.1) | copy-start | bytes 11010052

commit v3 on v2

--- a/solution.py
+++ b/solution.py
@@ -42,19 +42,18 @@
     pick = (jnp.arange(slot_total, dtype=jnp.int32)[:, None] == dest[None, :]).astype(
         jnp.bfloat16
     )
-    send_rows = jnp.dot(pick, tokens, preferred_element_type=jnp.float32).astype(jnp.bfloat16)
-    send_cot = jnp.dot(pick, cotangent, preferred_element_type=jnp.float32).astype(jnp.bfloat16)
-    send_rows = send_rows.reshape(n_experts, 1, most_rows, model_width)
-    send_cot = jnp.swapaxes(
-        send_cot.reshape(n_experts, most_rows, n_dp, half_width), 1, 2
-    )
-    packed = jnp.concatenate(
+    stacked = jnp.concatenate(
         [
-            jnp.broadcast_to(send_rows, (n_experts, n_dp, most_rows, model_width)),
-            send_cot,
+            jnp.broadcast_to(tokens[None], (n_dp, tok_rows, model_width)),
+            jnp.swapaxes(cotangent.reshape(tok_rows, n_dp, half_width), 0, 1),
         ],
-        axis=3,
-    ).reshape(n_experts * n_dp * most_rows, model_width + half_width)
+        axis=2,
+    ).reshape(n_dp * tok_rows, model_width + half_width)
+    pick_copy = (
+        pick.reshape(n_experts, 1, most_rows, 1, tok_rows)
+        * jnp.eye(n_dp, dtype=jnp.bfloat16).reshape(1, n_dp, 1, n_dp, 1)
+    ).reshape(n_experts * n_dp * most_rows, n_dp * tok_rows)
+    packed = jnp.dot(pick_copy, stacked, preferred_element_type=jnp.float32).astype(jnp.bfloat16)
     packed = packed.reshape(n_experts * n_dp, most_rows, model_width + half_width)
     got = lax.all_to_all(packed, ("expert", "dp"), split_axis=0, concat_axis=0, tiled=True)
     got_rows = got[:, :, :model_width]

time: 150 us -> 155 us (1.033)
  local copies, waits for them, and re-layouts: 12.6 us -> 17.4 us
  other arithmetic: 5.18 us -> 3.05 us
    reshape x1 -> x2, local copies, waits for them, and re-layouts: 0.37 us -> 8.35 us  [the longest x1 7.2 us: per_device(): packed.reshape(n_experts * n_dp, most_rows, model_width + half_width)]
    broadcast_in_dim x2 -> x1, local copies, waits for them, and re-layouts: 3.9 us -> 1.3 us  [per_device(): jnp.broadcast_to(tokens[None], (n_dp, tok_rows, model_width))]
    concatenate x1, other arithmetic: 2.59 us -> 0.26 us  [per_device(): jnp.concatenate([jnp.broadcast_to(tokens[None], (n_dp, tok_rows, model_wi...]
    dot_general x2 -> x1, matrix products: 1.86 us -> 3.2 us  [per_device(): jnp.dot(pick_copy, stacked, preferred_element_type=jnp.float32)]
where the time goes in v3:
time: 155 us; the launch traced here: 154 us
  blocking collectives  64.2 us (41%)
  waiting for transfers between devices  36.9 us (24%)
  matrix products  26 us (17%)
  local copies, waits for them, and re-layouts  17.4 us (11%)
  starting transfers between devices  5.62 us (4%)
  other arithmetic  3.05 us (2%)
    all_to_all x1, blocking collectives, per_device(): lax.all_to_all(packed, ('expert', 'dp'), split_axis=0, concat_axis=0, til...  64.2 us
    all_to_all x1, waiting for transfers between devices, per_device(): lax.all_to_all(back, ('expert', 'dp'), split_axis=0, concat_axis=0, tiled...  36.9 us
    reshape x1, local copies, waits for them, and re-layouts, per_device(): packed.reshape(n_experts * n_dp, most_rows, model_width + half_width)  7.2 us
    dot_general x1, matrix products, expert_math(): jnp.einsum('skd,skf->df', rows, d_gate, preferred_element_type=jnp.float32)  6.14 us
    all_to_all x1, starting transfers between devices, per_device(): lax.all_to_all(back, ('expert', 'dp'), split_axis=0, concat_axis=0, tiled...  5.62 us
    convert_element_type x1, local copies, waits for them, and re-layouts, expert_math(): back.astype(jnp.bfloat16)  4.67 us
    dot_general x1, matrix products, expert_math(): jnp.einsum('skf,df->skd', jnp.concatenate([d_gate, d_up], axis=2), jnp.co...  4.25 us
    dot_general x1, matrix products, expert_math(): jnp.einsum('skd,skf->df', rows, d_up, preferred_element_type=jnp.float32)  3.95 us
  transfers between devices with their start and end apart: 1, of which 1 were waited for; matrix products, arithmetic and copies ran while one was open for 7% of the time, Pallas kernels for 0%

profile of v3, /device:TPU:1, one launch (start us, length us, event | category | flops | bytes accessed | tf_op | source)
XLA Modules:
  0.0 153.9 jit_solution(9308036580700519688)
XLA Ops:
  0.7 0.7 fusion.43
  1.4 0.2 reduce_window_sum.11
  1.6 0.8 select_reduce_fusion
  2.4 0.7 add_add_fusion
  3.1 0.1 compare_convert_fusion
  3.2 0.1 copy.19
  3.2 1.2 reshape.90
  4.4 0.3 broadcast_multiply_fusion
  4.7 1.3 broadcast_in_dim.9
  6.0 0.3 pad_maximum_fusion
  6.3 3.2 %convolution_convert_fusion = bf16[512,4096]{1,0:T(8,128)(2,1)} fusion(bf16[256,4096]{1,0:T(8,128)(2,1)S(1)} %bitcast.53, bf16[64,8,2,128]{3,2,1,0:T(2,128)(2,1)S(1)} %bitcast.54), kind=kOutput, calls=%fused_computation.7 | convolution fusion | flops 1075838976 | bytes 6553600 | tf_op jit(solution)/shard_map/dot_general | solution.py:56
  9.5 7.2 %reshape.92 = bf16[128,4,4096]{2,1,0:T(4,128)(2,1)} reshape(bf16[512,4096]{1,0:T(8,128)(2,1)} %convolution_convert_fusion) | data formatting | bytes 8388608 | tf_op jit(solution)/shard_map/reshape | solution.py:57
  16.7 64.2 %all_to_all.10 = bf16[128,4,4096]{2,1,0:T(4,128)(2,1)S(1)} all-to-all(bf16[128,4,4096]{2,1,0:T(4,128)(2,1)} %reshape.92), channel_id=1, replica_groups=mesh['expert'=64,'dp'=2] {'expert','dp'}, dimensions={0} | all-to-all | bytes 8388608 | tf_op jit(solution)/shard_map/all_to_all | solution.py:58
  80.9 0.0 copy-start.3
  80.9 1.8 %slice.9 = bf16[128,4,3584]{2,1,0:T(4,128)(2,1)S(1)} slice(bf16[128,4,4096]{2,1,0:T(4,128)(2,1)S(1)} %all_to_all.10), slice={[0:128], [0:4], [0:3584]} | slice | bytes 7340032 | tf_op jit(solution)/shard_map/slice | solution.py:59
  82.7 0.0 copy-start
  82.7 0.3 slice.8
  83.0 0.0 copy-done.3
  83.0 0.0 copy-start.2
  83.0 2.3 %fusion.37 = (bf16[128,4,512]{2,0,1:T(8,128)(2,1)S(1)}, f32[128,4,512]{2,0,1:T(8,128)S(1)}) fusion(bf16[128,4,512]{2,1,0:T(4,128)(2,1)S(1)} %slice.8, bf16[1,3584,512]{2,1,0:T(8,128)(2,1)S(1)} %copy-done.3, bf16[128,4,3584]{2,1,0:T(4,128)(2,1)S(1)} %slice.9), kind=kOutput, calls=%fused_computation.28 | convolution fusion | flops 1880883200 | bytes 9437184 | tf_op jit(solution)/shard_map/skd,df->skf/dot_general | solution.py:8
  85.3 0.0 copy-done
  85.3 0.8 copy-done.2
  86.1 2.3 %fusion.31 = bf16[128,4,512]{2,0,1:T(8,128)(2,1)S(1)} fusion(bf16[1,3584,512]{2,1,0:T(8,128)(2,1)S(1)} %copy-done.2, bf16[128,4,3584]{2,1,0:T(4,128)(2,1)S(1)} %slice.9, f32[128,4,512]{2,0,1:T(8,128)S(1)} %get-tuple-element.4, bf16[128,4,512]{2,1,0:T(4,128)(2,1)S(1)} %slice.8), kind=kOutput, calls=%fused_computation.26 | convolution fusion | flops 1881931776 | bytes 9437184 | tf_op jit(solution)/shard_map/skd,df->skf/dot_general | solution.py:9
  88.4 4.3 %fusion.3 = bf16[128,4,3584]{2,0,1:T(8,128)(2,1)S(1)} fusion(bf16[3584,512]{1,0:T(8,128)(2,1)S(1)} %bitcast.59, bf16[3584,512]{1,0:T(8,128)(2,1)S(1)} %bitcast.60, bf16[128,4,512]{2,0,1:T(8,128)(2,1)S(1)} %get-tuple-element.3, bf16[128,4,512]{2,0,1:T(8,128)(2,1)S(1)} %fusion.31), kind=kOutput, calls=%fused_computation.6 | convolution fusion | flops 3776708608 | bytes 12058624 | tf_op jit(solution)/shard_map/skf,df->skd/dot_general | solution.py:16
  92.7 4.7 %copy.23 = bf16[128,4,3584]{2,1,0:T(4,128)(2,1)} copy(bf16[128,4,3584]{2,0,1:T(8,128)(2,1)S(1)} %fusion.3) | data formatting | bytes 7340032 | tf_op jit(solution)/shard_map/convert_element_type | solution.py:24
  97.3 5.6 %all-to-all-start.1 = ((bf16[128,4,3584]{2,1,0:T(4,128)(2,1)}), bf16[128,4,3584]{2,1,0:T(4,128)(2,1)}, u32[]{:S(2)}, u32[]{:S(2)}) async-start(bf16[128,4,3584]{2,1,0:T(4,128)(2,1)} %copy.23), calls=%async_computation.1 | async-start | bytes 7340032 | tf_op jit(solution)/shard_map/all_to_all | solution.py:64
  103.0 0.0 copy-start.1
  103.0 6.1 %fusion.4 = bf16[1,3584,512]{2,1,0:T(8,128)(2,1)} fusion(bf16[128,4,512]{2,0,1:T(8,128)(2,1)S(1)} %fusion.31, bf16[128,4,3584]{2,1,0:T(4,128)(2,1)} %copy-done), kind=kOutput, calls=%fused_computation.8 | convolution fusion | flops 1880883200 | bytes 7864320 | tf_op jit(solution)/shard_map/skd,skf->df/dot_general | solution.py:22
  109.1 0.0 copy-done.1
  109.1 3.9 %fusion.5 = bf16[1,3584,512]{2,1,0:T(8,128)(2,1)} fusion(bf16[128,4,512]{2,0,1:T(8,128)(2,1)S(1)} %get-tuple-element.3, bf16[128,4,3584]{2,1,0:T(4,128)(2,1)S(1)} %copy-done.1), kind=kOutput, calls=%fused_computation.9 | convolution fusion | flops 1880883200 | bytes 7864320 | tf_op jit(solution)/shard_map/skd,skf->df/dot_general | solution.py:23
  113.1 36.9 %all-to-all-done.1 = bf16[128,4,3584]{2,1,0:T(4,128)(2,1)} async-done(((bf16[128,4,3584]{2,1,0:T(4,128)(2,1)}), bf16[128,4,3584]{2,1,0:T(4,128)(2,1)}, u32[]{:S(2)}, u32[]{:S(2)}) %all-to-all-start.1) | async-done | bytes 3670048 | tf_op jit(solution)/shard_map/all_to_all | solution.py:64
  149.9 0.1 broadcast_in_dim.8
  150.0 3.9 %fusion.6 = bf16[128,3584]{1,0:T(8,128)(2,1)} fusion(bf16[128,4,128]{2,0,1:T(8,128)(2,1)S(1)} %bitcast.56, bf16[128,4,3584]{2,1,0:T(4,128)(2,1)} %all-to-all-done.1), kind=kOutput, calls=%fused_computation.11 | convolution fusion | flops 470220800 | bytes 4718592 | tf_op jit(solution)/shard_map/dot_general | solution.py:68
  (3 shorter events, 0.0 us)
Async XLA Ops:
  80.9 2.1 %copy-start.3 = (bf16[1,3584,512]{2,1,0:T(8,128)(2,1)S(1)}, bf16[1,3584,512]{2,1,0:T(8,128)(2,1)}, u32[]{:S(2)}) copy-start(bf16[1,3584,512]{2,1,0:T(8,128)(2,1)} %param.8) | copy-start | bytes 11010052
  82.7 2.6 %copy-start = (bf16[128,4,3584]{2,1,0:T(4,128)(2,1)}, bf16[128,4,3584]{2,1,0:T(4,128)(2,1)S(1)}, u32[]{:S(2)}) copy-start(bf16[128,4,3584]{2,1,0:T(4,128)(2,1)S(1)} %slice.9) | copy-start | bytes 11010052
  83.0 3.1 %copy-start.2 = (bf16[1,3584,512]{2,1,0:T(8,128)(2,1)S(1)}, bf16[1,3584,512]{2,1,0:T(8,128)(2,1)}, u32[]{:S(2)}) copy-start(bf16[1,3584,512]{2,1,0:T(8,128)(2,1)} %param.9) | copy-start | bytes 11010052
  97.3 52.6 %all-to-all-start.1 = ((bf16[128,4,3584]{2,1,0:T(4,128)(2,1)}), bf16[128,4,3584]{2,1,0:T(4,128)(2,1)}, u32[]{:S(2)}, u32[]{:S(2)}) async-start(bf16[128,4,3584]{2,1,0:T(4,128)(2,1)} %copy.23), calls=%async_computation.1 | async-start | bytes 7340032 | tf_op jit(solution)/shard_map/all_to_all | solution.py:64
  103.0 6.2 %copy-start.1 = (bf16[128,4,3584]{2,1,0:T(4,128)(2,1)S(1)}, bf16[128,4,3584]{2,1,0:T(4,128)(2,1)}, u32[]{:S(2)}) copy-start(bf16[128,4,3584]{2,1,0:T(4,128)(2,1)} %copy-done) | copy-start | bytes 11010052

commit v4 on v2

--- a/solution.py
+++ b/solution.py
@@ -21,7 +21,7 @@
     )
     grad_g = jnp.einsum("skd,skf->df", rows, d_gate, preferred_element_type=jnp.float32)
     grad_u = jnp.einsum("skd,skf->df", rows, d_up, preferred_element_type=jnp.float32)
-    return back.astype(jnp.bfloat16), grad_g.astype(jnp.bfloat16), grad_u.astype(jnp.bfloat16)
+    return back, grad_g.astype(jnp.bfloat16), grad_u.astype(jnp.bfloat16)
 
 
 def per_device(tokens, cotangent, routing, w_gate, w_up):
@@ -67,7 +67,11 @@
         pick.reshape(n_experts, 1, most_rows, tok_rows), (n_experts, n_dp, most_rows, tok_rows)
     ).reshape(n_experts * n_dp, most_rows, tok_rows)
     grad_tokens = lax.dot_general(
-        pick_dup, returned, (((0, 1), (0, 1)), ((), ())), preferred_element_type=jnp.float32
+        pick_dup.astype(jnp.float32),
+        returned,
+        (((0, 1), (0, 1)), ((), ())),
+        precision=lax.Precision.HIGHEST,
+        preferred_element_type=jnp.float32,
     ).astype(jnp.bfloat16)
     return grad_tokens, grad_g[None], grad_u[None]
 

time: 150 us -> 201 us (1.34)
  waiting for transfers between devices: 36.8 us -> 78.9 us
  matrix products: 24.6 us -> 29 us
  local copies, waits for them, and re-layouts: 12.6 us -> 16.7 us
    all_to_all x1, waiting for transfers between devices: 36.8 us -> 78.9 us  [per_device(): lax.all_to_all(back, ('expert', 'dp'), split_axis=0, concat_axis=0, tiled...]
    dot_general x0 -> x1, local copies, waits for them, and re-layouts: none -> 7.96 us  [expert_math(): jnp.einsum('skf,df->skd', jnp.concatenate([d_gate, d_up], axis=2), jnp.co...]
    dot_general x1, matrix products: 3.89 us -> 8.58 us  [per_device(): lax.dot_general(pick_dup.astype(jnp.float32), returned, (((0, 1), (0, 1))...]
    convert_element_type x1 -> x0, local copies, waits for them, and re-layouts: 4.67 us -> none  [expert_math(): back.astype(jnp.bfloat16)]
  transfers between devices with their start and end apart: 1 -> 1, of which waited for: 1 -> 1; matrix products, arithmetic and copies ran while one was open for 7% -> 5% of each run, Pallas kernels for 0% -> 0%
where the time goes in v4:
time: 201 us; the launch traced here: 200 us
  waiting for transfers between devices  78.9 us (39%)
  blocking collectives  64 us (32%)
  matrix products  29 us (14%)
  local copies, waits for them, and re-layouts  16.7 us (8%)
  starting transfers between devices  5.82 us (3%)
  other arithmetic  5.18 us (3%)
    all_to_all x1, waiting for transfers between devices, per_device(): lax.all_to_all(back, ('expert', 'dp'), split_axis=0, concat_axis=0, tiled...  78.9 us
    all_to_all x1, blocking collectives, per_device(): lax.all_to_all(packed, ('expert', 'dp'), split_axis=0, concat_axis=0, til...  64 us
    dot_general x1, matrix products, per_device(): lax.dot_general(pick_dup.astype(jnp.float32), returned, (((0, 1), (0, 1))...  8.58 us
    dot_general x1, local copies, waits for them, and re-layouts, expert_math(): jnp.einsum('skf,df->skd', jnp.concatenate([d_gate, d_up], axis=2), jnp.co...  7.96 us
    dot_general x1, matrix products, expert_math(): jnp.einsum('skd,skf->df', rows, d_gate, preferred_element_type=jnp.float32)  6.14 us
    all_to_all x1, starting transfers between devices, per_device(): lax.all_to_all(back, ('expert', 'dp'), split_axis=0, concat_axis=0, tiled...  5.82 us
  transfers between devices with their start and end apart: 1, of which 1 were waited for; matrix products, arithmetic and copies ran while one was open for 5% of the time, Pallas kernels for 0%

profile of v4, /device:TPU:1, one launch (start us, length us, event | category | flops | bytes accessed | tf_op | source)
XLA Modules:
  0.0 200.5 jit_solution(12223248451910547346)
XLA Ops:
  0.6 0.0 copy-start
  0.6 0.8 fusion.48
  1.5 0.2 reduce_window_sum.11
  1.6 0.8 select_reduce_fusion
  2.5 0.7 add_add_fusion
  3.1 1.2 convolution_convert_fusion.1
  4.4 0.4 reshape.43
  4.8 0.2 copy.17
  5.0 0.0 copy-done
  5.0 0.6 convolution_convert_fusion
  5.6 1.5 broadcast_in_dim.22
  7.1 2.4 %broadcast_in_dim.23 = bf16[64,2,4,3584]{3,2,1,0:T(4,128)(2,1)S(1)} broadcast(bf16[64,4,3584]{2,1,0:T(4,128)(2,1)} %broadcast_in_dim.22), dimensions={0,2,3} | broadcast | bytes 5505024 | tf_op jit(solution)/shard_map/broadcast_in_dim | solution.py:53
  9.5 2.6 %pad_maximum_fusion = bf16[64,2,4,4096]{3,2,1,0:T(4,128)(2,1)S(1)} fusion(bf16[64,2,4,512]{3,2,1,0:T(4,128)(2,1)S(1)} %copy.17, bf16[64,2,4,3584]{3,2,1,0:T(4,128)(2,1)S(1)} %broadcast_in_dim.23), kind=kLoop, calls=%fused_computation.13 | loop fusion | flops 8388608 | bytes 8388608 | tf_op jit(solution)/shard_map/concatenate | solution.py:51
  12.1 64.0 %all_to_all.10 = bf16[128,4,4096]{2,1,0:T(4,128)(2,1)S(1)} all-to-all(bf16[128,4,4096]{2,1,0:T(4,128)(2,1)S(1)} %bitcast.47), channel_id=1, replica_groups=mesh['expert'=64,'dp'=2] {'expert','dp'}, dimensions={0} | all-to-all | bytes 8388608 | tf_op jit(solution)/shard_map/all_to_all | solution.py:59
  76.1 0.3 slice.8
  76.4 0.0 copy-start.4
  76.4 1.8 slice.9
  78.2 0.2 copy-done.4
  78.4 0.0 copy-start.1
  78.4 0.0 copy-start.3
  78.4 2.2 %fusion.42 = (bf16[128,4,512]{2,0,1:T(8,128)(2,1)S(1)}, f32[128,4,512]{2,0,1:T(8,128)S(1)}) fusion(bf16[128,4,512]{2,1,0:T(4,128)(2,1)S(1)} %slice.8, bf16[1,3584,512]{2,1,0:T(8,128)(2,1)S(1)} %copy-done.4, bf16[128,4,3584]{2,1,0:T(4,128)(2,1)S(1)} %slice.9), kind=kOutput, calls=%fused_computation.29 | convolution fusion | flops 1880883200 | bytes 9437184 | tf_op jit(solution)/shard_map/skd,df->skf/dot_general | solution.py:8
  80.7 0.0 copy-done.1
  80.7 1.1 copy-done.3
  81.8 2.3 %fusion.36 = bf16[128,4,512]{2,0,1:T(8,128)(2,1)S(1)} fusion(bf16[1,3584,512]{2,1,0:T(8,128)(2,1)S(1)} %copy-done.3, bf16[128,4,3584]{2,1,0:T(4,128)(2,1)S(1)} %slice.9, f32[128,4,512]{2,0,1:T(8,128)S(1)} %get-tuple-element.4, bf16[128,4,512]{2,1,0:T(4,128)(2,1)S(1)} %slice.8), kind=kOutput, calls=%fused_computation.26 | convolution fusion | flops 1881931776 | bytes 9437184 | tf_op jit(solution)/shard_map/skd,df->skf/dot_general | solution.py:9
  84.1 0.0 copy-start.5
  84.1 0.8 copy-done.5
  84.9 4.0 %fusion = f32[128,4,3584]{2,0,1:T(8,128)S(1)} fusion(bf16[3584,512]{1,0:T(8,128)(2,1)S(1)} %bitcast.52, bf16[3584,512]{1,0:T(8,128)(2,1)S(1)} %bitcast.53, bf16[128,4,512]{2,0,1:T(8,128)(2,1)S(1)} %get-tuple-element.3, bf16[128,4,512]{2,0,1:T(8,128)(2,1)S(1)} %fusion.36), kind=kOutput, calls=%fused_computation.1 | convolution fusion | flops 3774873600 | bytes 15728640 | tf_op jit(solution)/shard_map/skf,df->skd/dot_general | solution.py:16
  88.9 8.0 %copy.20 = f32[128,4,3584]{2,1,0:T(4,128)} copy(f32[128,4,3584]{2,0,1:T(8,128)S(1)} %fusion) | data formatting | bytes 14680064 | tf_op jit(solution)/shard_map/skf,df->skd/dot_general | solution.py:16
  96.9 0.0 copy-start.6
  96.9 5.8 %all-to-all-start.1 = ((f32[128,4,3584]{2,1,0:T(4,128)}), f32[128,4,3584]{2,1,0:T(4,128)}, u32[]{:S(2)}, u32[]{:S(2)}) async-start(f32[128,4,3584]{2,1,0:T(4,128)} %copy.20), calls=%async_computation.1 | async-start | bytes 14680064 | tf_op jit(solution)/shard_map/all_to_all | solution.py:65
  102.7 0.1 compare_convert_fusion
  102.8 0.0 copy-done.6
  102.8 0.0 copy-start.2
  102.8 6.1 %fusion.5 = bf16[1,3584,512]{2,1,0:T(8,128)(2,1)} fusion(bf16[128,4,512]{2,0,1:T(8,128)(2,1)S(1)} %copy-done.6, bf16[128,4,3584]{2,1,0:T(4,128)(2,1)} %copy-done.1), kind=kOutput, calls=%fused_computation.8 | convolution fusion | flops 1880883200 | bytes 7864320 | tf_op jit(solution)/shard_map/skd,skf->df/dot_general | solution.py:22
  109.0 0.0 copy-done.2
  109.0 3.9 %fusion.6 = bf16[1,3584,512]{2,1,0:T(8,128)(2,1)} fusion(bf16[128,4,512]{2,0,1:T(8,128)(2,1)S(1)} %get-tuple-element.3, bf16[128,4,3584]{2,1,0:T(4,128)(2,1)S(1)} %copy-done.2), kind=kOutput, calls=%fused_computation.9 | convolution fusion | flops 1880883200 | bytes 7864320 | tf_op jit(solution)/shard_map/skd,skf->df/dot_general | solution.py:23
  112.9 78.9 %all-to-all-done.1 = f32[128,4,3584]{2,1,0:T(4,128)} async-done(((f32[128,4,3584]{2,1,0:T(4,128)}), f32[128,4,3584]{2,1,0:T(4,128)}, u32[]{:S(2)}, u32[]{:S(2)}) %all-to-all-start.1) | async-done | bytes 7340064 | tf_op jit(solution)/shard_map/all_to_all | solution.py:65
  191.8 0.1 broadcast_in_dim.10
  191.9 8.6 %fusion.10 = bf16[128,3584]{1,0:T(8,128)(2,1)} fusion(bf16[128,4,128]{2,0,1:T(8,128)(2,1)S(1)} %bitcast.49, f32[128,4,3584]{2,1,0:T(4,128)} %all-to-all-done.1), kind=kOutput, calls=%fused_computation.12 | convolution fusion | flops 2819031040 | bytes 8388608 | tf_op jit(solution)/shard_map/dot_general | solution.py:69
  (1 shorter events, 0.0 us)
Async XLA Ops:
  0.6 4.3 %copy-start = (bf16[128,3584]{1,0:T(8,128)(2,1)S(1)}, bf16[128,3584]{1,0:T(8,128)(2,1)}, u32[]{:S(2)}) copy-start(bf16[128,3584]{1,0:T(8,128)(2,1)} %param.5) | copy-start | bytes 2752516
  76.4 2.0 %copy-start.4 = (bf16[1,3584,512]{2,1,0:T(8,128)(2,1)S(1)}, bf16[1,3584,512]{2,1,0:T(8,128)(2,1)}, u32[]{:S(2)}) copy-start(bf16[1,3584,512]{2,1,0:T(8,128)(2,1)} %param.8) | copy-start | bytes 11010052
  78.4 2.2 %copy-start.1 = (bf16[128,4,3584]{2,1,0:T(4,128)(2,1)}, bf16[128,4,3584]{2,1,0:T(4,128)(2,1)S(1)}, u32[]{:S(2)}) copy-start(bf16[128,4,3584]{2,1,0:T(4,128)(2,1)S(1)} %slice.9) | copy-start | bytes 11010052
  78.4 3.4 %copy-start.3 = (bf16[1,3584,512]{2,1,0:T(8,128)(2,1)S(1)}, bf16[1,3584,512]{2,1,0:T(8,128)(2,1)}, u32[]{:S(2)}) copy-start(bf16[1,3584,512]{2,1,0:T(8,128)(2,1)} %param.9) | copy-start | bytes 11010052
  84.1 0.8 copy-start.5
  96.9 6.0 %copy-start.6 = (bf16[128,4,512]{2,0,1:T(8,128)(2,1)S(1)}, bf16[128,4,512]{2,0,1:T(8,128)(2,1)}, u32[]{:S(2)}) copy-start(bf16[128,4,512]{2,0,1:T(8,128)(2,1)} %copy-done.5) | copy-start | bytes 1572868
  96.9 95.0 %all-to-all-start.1 = ((f32[128,4,3584]{2,1,0:T(4,128)}), f32[128,4,3584]{2,1,0:T(4,128)}, u32[]{:S(2)}, u32[]{:S(2)}) async-start(f32[128,4,3584]{2,1,0:T(4,128)} %copy.20), calls=%async_computation.1 | async-start | bytes 14680064 | tf_op jit(solution)/shard_map/all_to_all | solution.py:65
  102.8 6.2 %copy-start.2 = (bf16[128,4,3584]{2,1,0:T(4,128)(2,1)S(1)}, bf16[128,4,3584]{2,1,0:T(4,128)(2,1)}, u32[]{:S(2)}) copy-start(bf16[128,4,3584]{2,1,0:T(4,128)(2,1)} %copy-done.1) | copy-start | bytes 11010052

commit v5 on v2

--- a/solution.py
+++ b/solution.py
@@ -5,8 +5,15 @@
 
 
 def expert_math(rows, cot, weight_gate, weight_up):
-    gate_act = jnp.einsum("skd,df->skf", rows, weight_gate, preferred_element_type=jnp.float32)
-    up_act = jnp.einsum("skd,df->skf", rows, weight_up, preferred_element_type=jnp.float32)
+    half_width = weight_gate.shape[1]
+    both_act = jnp.einsum(
+        "skd,df->skf",
+        rows,
+        jnp.concatenate([weight_gate, weight_up], axis=1),
+        preferred_element_type=jnp.float32,
+    )
+    gate_act = both_act[:, :, :half_width]
+    up_act = both_act[:, :, half_width:]
     sigmoid_gate = jax.nn.sigmoid(gate_act)
     cot_float = cot.astype(jnp.float32)
     d_up = (cot_float * gate_act * sigmoid_gate).astype(jnp.bfloat16)

time: 150 us -> 150 us (level)
    dot_general x1, matrix products: 6.14 us -> 3.94 us  [expert_math(): jnp.einsum('skd,skf->df', rows, d_gate, preferred_element_type=jnp.float32)]
    dot_general x1, matrix products: 3.95 us -> 6.14 us  [expert_math(): jnp.einsum('skd,skf->df', rows, d_up, preferred_element_type=jnp.float32)]
    dot_general x2 -> x1, matrix products: 4.54 us -> 3.98 us  [expert_math(): jnp.einsum('skd,df->skf', rows, jnp.concatenate([weight_gate, weight_up],...]
where the time goes in v5:
time: 150 us
  blocking collectives  64 us (43%)
  waiting for transfers between devices  36.8 us (25%)
  matrix products  23.9 us (16%)
  local copies, waits for them, and re-layouts  13 us (9%)
  other arithmetic  5.75 us (4%)
  starting transfers between devices  5.62 us (4%)
    all_to_all x1, blocking collectives, per_device(): lax.all_to_all(packed, ('expert', 'dp'), split_axis=0, concat_axis=0, til...  64 us
    all_to_all x1, waiting for transfers between devices, per_device(): lax.all_to_all(back, ('expert', 'dp'), split_axis=0, concat_axis=0, tiled...  36.8 us
    dot_general x1, matrix products, expert_math(): jnp.einsum('skd,skf->df', rows, d_up, preferred_element_type=jnp.float32)  6.14 us
    all_to_all x1, starting transfers between devices, per_device(): lax.all_to_all(back, ('expert', 'dp'), split_axis=0, concat_axis=0, tiled...  5.62 us
    convert_element_type x1, local copies, waits for them, and re-layouts, expert_math(): back.astype(jnp.bfloat16)  4.68 us
    dot_general x1, matrix products, expert_math(): jnp.einsum('skf,df->skd', jnp.concatenate([d_gate, d_up], axis=2), jnp.co...  4.25 us
    dot_general x1, matrix products, expert_math(): jnp.einsum('skd,df->skf', rows, jnp.concatenate([weight_gate, weight_up],...  3.98 us
    dot_general x1, matrix products, expert_math(): jnp.einsum('skd,skf->df', rows, d_gate, preferred_element_type=jnp.float32)  3.94 us
  transfers between devices with their start and end apart: 1, of which 1 were waited for; matrix products, arithmetic and copies ran while one was open for 7% of the time, Pallas kernels for 0%

profile of v5, /device:TPU:1, one launch (start us, length us, event | category | flops | bytes accessed | tf_op | source)
XLA Modules:
  0.0 149.8 jit_solution(15834004592861523954)
XLA Ops:
  0.6 0.0 copy-start
  0.6 0.0 copy-start.4
  0.7 0.8 fusion.18
  1.5 0.2 reduce_window_sum.11
  1.7 0.8 select_reduce_fusion
  2.5 0.7 add_add_fusion
  3.2 0.0 copy-done
  3.2 0.6 convolution_convert_fusion.1
  3.8 1.5 broadcast_in_dim.22
  5.2 0.0 copy-done.4
  5.2 0.0 copy-start.1
  5.2 1.1 convolution_convert_fusion.2
  6.3 1.4 reshape.43
  7.8 0.2 copy.17
  8.0 0.0 copy-done.1
  8.0 0.9 broadcast_in_dim.23
  8.9 2.6 %pad_maximum_fusion = bf16[64,2,4,4096]{3,2,1,0:T(4,128)(2,1)S(1)} fusion(bf16[64,2,4,512]{3,2,1,0:T(4,128)(2,1)S(1)} %copy.17, bf16[64,2,4,3584]{3,2,1,0:T(4,128)(2,1)S(1)} %broadcast_in_dim.23), kind=kLoop, calls=%fused_computation.10 | loop fusion | flops 8388608 | bytes 8388608 | tf_op jit(solution)/shard_map/concatenate | solution.py:58
  11.6 64.0 %all_to_all.10 = bf16[128,4,4096]{2,1,0:T(4,128)(2,1)S(1)} all-to-all(bf16[128,4,4096]{2,1,0:T(4,128)(2,1)S(1)} %bitcast.32), channel_id=1, replica_groups=mesh['expert'=64,'dp'=2] {'expert','dp'}, dimensions={0} | all-to-all | bytes 8388608 | tf_op jit(solution)/shard_map/all_to_all | solution.py:66
  75.6 0.0 copy-start.5
  75.6 0.0 copy-start.6
  75.6 1.8 %slice.17 = bf16[128,4,3584]{2,1,0:T(4,128)(2,1)S(1)} slice(bf16[128,4,4096]{2,1,0:T(4,128)(2,1)S(1)} %all_to_all.10), slice={[0:128], [0:4], [0:3584]} | slice | bytes 7340032 | tf_op jit(solution)/shard_map/slice | solution.py:67
  77.4 0.0 copy-start.2
  77.4 0.2 copy-done.5
  77.6 1.9 %copy-done.6 = bf16[1,3584,512]{2,1,0:T(8,128)(2,1)S(1)} copy-done((bf16[1,3584,512]{2,1,0:T(8,128)(2,1)S(1)}, bf16[1,3584,512]{2,1,0:T(8,128)(2,1)}, u32[]{:S(2)}) %copy-start.6) | copy-done | bytes 3670040
  79.5 4.0 %fusion.3 = f32[128,4,1024]{2,0,1:T(8,128)S(1)} fusion(bf16[3584,512]{1,0:T(8,128)(2,1)S(1)} %bitcast.37, bf16[3584,512]{1,0:T(8,128)(2,1)S(1)} %bitcast.39, bf16[128,4,3584]{2,1,0:T(4,128)(2,1)S(1)} %slice.17), kind=kOutput, calls=%fused_computation.9 | convolution fusion | flops 3772776448 | bytes 13107200 | tf_op jit(solution)/shard_map/skd,df->skf/dot_general | solution.py:9
  83.5 0.0 copy-done.2
  83.5 0.3 slice.16
  83.8 0.5 fusion.10
  84.3 4.3 %convolution_convert_fusion = bf16[128,4,3584]{2,0,1:T(8,128)(2,1)S(1)} fusion(bf16[3584,512]{1,0:T(8,128)(2,1)S(1)} %bitcast.38, bf16[3584,512]{1,0:T(8,128)(2,1)S(1)} %bitcast.40, bf16[128,4,512]{2,0,1:T(8,128)(2,1)S(1)} %get-tuple-element.4, bf16[128,4,512]{2,0,1:T(8,128)(2,1)S(1)} %get-tuple-element.3), kind=kOutput, calls=%fused_computation.3 | convolution fusion | flops 3776708608 | bytes 12058624 | tf_op jit(solution)/shard_map/skf,df->skd/dot_general | solution.py:23
  88.6 4.7 %copy.20 = bf16[128,4,3584]{2,1,0:T(4,128)(2,1)} copy(bf16[128,4,3584]{2,0,1:T(8,128)(2,1)S(1)} %convolution_convert_fusion) | data formatting | bytes 7340032 | tf_op jit(solution)/shard_map/convert_element_type | solution.py:31
  93.3 5.6 %all-to-all-start.1 = ((bf16[128,4,3584]{2,1,0:T(4,128)(2,1)}), bf16[128,4,3584]{2,1,0:T(4,128)(2,1)}, u32[]{:S(2)}, u32[]{:S(2)}) async-start(bf16[128,4,3584]{2,1,0:T(4,128)(2,1)} %copy.20), calls=%async_computation.1 | async-start | bytes 7340032 | tf_op jit(solution)/shard_map/all_to_all | solution.py:72
  98.9 0.1 compare_convert_fusion
  99.0 0.0 copy-start.3
  99.0 6.1 %fusion.1 = bf16[1,3584,512]{2,1,0:T(8,128)(2,1)} fusion(bf16[128,4,512]{2,0,1:T(8,128)(2,1)S(1)} %get-tuple-element.4, bf16[128,4,3584]{2,1,0:T(4,128)(2,1)} %copy-done.2), kind=kOutput, calls=%fused_computation.5 | convolution fusion | flops 1880883200 | bytes 7864320 | tf_op jit(solution)/shard_map/skd,skf->df/dot_general | solution.py:30
  105.2 0.0 copy-done.3
  105.2 3.9 %fusion = bf16[1,3584,512]{2,1,0:T(8,128)(2,1)} fusion(bf16[128,4,512]{2,0,1:T(8,128)(2,1)S(1)} %get-tuple-element.3, bf16[128,4,3584]{2,1,0:T(4,128)(2,1)S(1)} %copy-done.3), kind=kOutput, calls=%fused_computation.4 | convolution fusion | flops 1880883200 | bytes 7864320 | tf_op jit(solution)/shard_map/skd,skf->df/dot_general | solution.py:29
  109.1 36.8 %all-to-all-done.1 = bf16[128,4,3584]{2,1,0:T(4,128)(2,1)} async-done(((bf16[128,4,3584]{2,1,0:T(4,128)(2,1)}), bf16[128,4,3584]{2,1,0:T(4,128)(2,1)}, u32[]{:S(2)}, u32[]{:S(2)}) %all-to-all-start.1) | async-done | bytes 3670048 | tf_op jit(solution)/shard_map/all_to_all | solution.py:72
  145.9 0.1 broadcast_in_dim.10
  145.9 3.9 %fusion.2 = bf16[128,3584]{1,0:T(8,128)(2,1)} fusion(bf16[128,4,128]{2,0,1:T(8,128)(2,1)S(1)} %bitcast.34, bf16[128,4,3584]{2,1,0:T(4,128)(2,1)} %all-to-all-done.1), kind=kOutput, calls=%fused_computation.8 | convolution fusion | flops 470220800 | bytes 4718592 | tf_op jit(solution)/shard_map/dot_general | solution.py:76
  (1 shorter events, 0.0 us)
Async XLA Ops:
  0.6 2.5 %copy-start = (bf16[128,3584]{1,0:T(8,128)(2,1)S(1)}, bf16[128,3584]{1,0:T(8,128)(2,1)}, u32[]{:S(2)}) copy-start(bf16[128,3584]{1,0:T(8,128)(2,1)} %param.5) | copy-start | bytes 2752516
  0.6 4.6 %copy-start.4 = (bf16[128,1024]{1,0:T(8,128)(2,1)S(1)}, bf16[128,1024]{1,0:T(8,128)(2,1)}, u32[]{:S(2)}) copy-start(bf16[128,1024]{1,0:T(8,128)(2,1)} %param.6) | copy-start | bytes 786436
  5.2 2.7 %copy-start.1 = (bf16[64,4,3584]{2,1,0:T(4,128)(2,1)S(1)}, bf16[64,4,3584]{2,1,0:T(4,128)(2,1)}, u32[]{:S(2)}) copy-start(bf16[64,4,3584]{2,1,0:T(4,128)(2,1)} %broadcast_in_dim.22) | copy-start | bytes 5505028
  75.6 2.0 %copy-start.5 = (bf16[1,3584,512]{2,1,0:T(8,128)(2,1)S(1)}, bf16[1,3584,512]{2,1,0:T(8,128)(2,1)}, u32[]{:S(2)}) copy-start(bf16[1,3584,512]{2,1,0:T(8,128)(2,1)} %param.9) | copy-start | bytes 11010052
  75.6 3.9 %copy-start.6 = (bf16[1,3584,512]{2,1,0:T(8,128)(2,1)S(1)}, bf16[1,3584,512]{2,1,0:T(8,128)(2,1)}, u32[]{:S(2)}) copy-start(bf16[1,3584,512]{2,1,0:T(8,128)(2,1)} %param.8) | copy-start | bytes 11010052
  77.4 6.1 %copy-start.2 = (bf16[128,4,3584]{2,1,0:T(4,128)(2,1)}, bf16[128,4,3584]{2,1,0:T(4,128)(2,1)S(1)}, u32[]{:S(2)}) copy-start(bf16[128,4,3584]{2,1,0:T(4,128)(2,1)S(1)} %slice.17) | copy-start | bytes 11010052
  93.3 52.6 %all-to-all-start.1 = ((bf16[128,4,3584]{2,1,0:T(4,128)(2,1)}), bf16[128,4,3584]{2,1,0:T(4,128)(2,1)}, u32[]{:S(2)}, u32[]{:S(2)}) async-start(bf16[128,4,3584]{2,1,0:T(4,128)(2,1)} %copy.20), calls=%async_computation.1 | async-start | bytes 7340032 | tf_op jit(solution)/shard_map/all_to_all | solution.py:72
  99.0 6.2 %copy-start.3 = (bf16[128,4,3584]{2,1,0:T(4,128)(2,1)S(1)}, bf16[128,4,3584]{2,1,0:T(4,128)(2,1)}, u32[]{:S(2)}) copy-start(bf16[128,4,3584]{2,1,0:T(4,128)(2,1)} %copy-done.2) | copy-start | bytes 11010052

commit v6 on v2

--- a/solution.py
+++ b/solution.py
@@ -34,10 +34,11 @@
     slot_total = n_experts * most_rows
 
     expert_of = routing[:, 0]
-    one_hot = (expert_of[:, None] == jnp.arange(n_experts, dtype=jnp.int32)[None, :]).astype(
-        jnp.int32
-    )
-    slot_of = jnp.sum(jnp.cumsum(one_hot, axis=0) * one_hot, axis=1) - 1
+    same = expert_of[:, None] == expert_of[None, :]
+    earlier = jnp.arange(tok_rows, dtype=jnp.int32)[None, :] < jnp.arange(
+        tok_rows, dtype=jnp.int32
+    )[:, None]
+    slot_of = jnp.sum((same & earlier).astype(jnp.int32), axis=1)
     dest = expert_of * most_rows + slot_of
     pick = (jnp.arange(slot_total, dtype=jnp.int32)[:, None] == dest[None, :]).astype(
         jnp.bfloat16

time: 150 us -> 148 us (0.987)
  no operation moved by 1% of the time
where the time goes in v6:
time: 148 us
  blocking collectives  64 us (43%)
  waiting for transfers between devices  36.8 us (25%)
  matrix products  24.5 us (17%)
  local copies, waits for them, and re-layouts  11.7 us (8%)
  starting transfers between devices  5.61 us (4%)
  other arithmetic  4.31 us (3%)
    all_to_all x1, blocking collectives, per_device(): lax.all_to_all(packed, ('expert', 'dp'), split_axis=0, concat_axis=0, til...  64 us
    all_to_all x1, waiting for transfers between devices, per_device(): lax.all_to_all(back, ('expert', 'dp'), split_axis=0, concat_axis=0, tiled...  36.8 us
    dot_general x1, matrix products, expert_math(): jnp.einsum('skd,skf->df', rows, d_gate, preferred_element_type=jnp.float32)  6.14 us
    all_to_all x1, starting transfers between devices, per_device(): lax.all_to_all(back, ('expert', 'dp'), split_axis=0, concat_axis=0, tiled...  5.61 us
    convert_element_type x1, local copies, waits for them, and re-layouts, expert_math(): back.astype(jnp.bfloat16)  4.66 us
    dot_general x1, matrix products, expert_math(): jnp.einsum('skf,df->skd', jnp.concatenate([d_gate, d_up], axis=2), jnp.co...  4.25 us
    dot_general x1, matrix products, expert_math(): jnp.einsum('skd,skf->df', rows, d_up, preferred_element_type=jnp.float32)  3.95 us
    dot_general x1, matrix products, per_device(): lax.dot_general(pick_dup, returned, (((0, 1), (0, 1)), ((), ())), preferr...  3.89 us
  transfers between devices with their start and end apart: 1, of which 1 were waited for; matrix products, arithmetic and copies ran while one was open for 7% of the time, Pallas kernels for 0%

profile of v6, /device:TPU:1, one launch (start us, length us, event | category | flops | bytes accessed | tf_op | source)
XLA Modules:
  0.0 147.6 jit_solution(10302109981443899708)
XLA Ops:
  0.6 0.0 copy-start
  0.6 0.0 copy-start.4
  0.7 0.9 convert_reduce_fusion
  1.6 0.7 multiply_add_fusion.1
  2.3 0.0 copy-done
  2.3 0.6 convolution_convert_fusion
  2.9 1.5 broadcast_in_dim.11
  4.3 0.0 copy-done.4
  4.3 0.0 copy-start.1
  4.3 1.1 convolution_convert_fusion.1
  5.4 1.4 reshape.43
  6.9 0.2 copy.25
  7.1 0.0 copy-done.1
  7.1 0.9 broadcast_in_dim.24
  8.0 2.6 %pad_maximum_fusion = bf16[64,2,4,4096]{3,2,1,0:T(4,128)(2,1)S(1)} fusion(bf16[64,2,4,512]{3,2,1,0:T(4,128)(2,1)S(1)} %copy.25, bf16[64,2,4,3584]{3,2,1,0:T(4,128)(2,1)S(1)} %broadcast_in_dim.24), kind=kLoop, calls=%fused_computation.12 | loop fusion | flops 8388608 | bytes 8388608 | tf_op jit(solution)/shard_map/concatenate | solution.py:52
  10.7 64.0 %all_to_all.10 = bf16[128,4,4096]{2,1,0:T(4,128)(2,1)S(1)} all-to-all(bf16[128,4,4096]{2,1,0:T(4,128)(2,1)S(1)} %bitcast.49), channel_id=1, replica_groups=mesh['expert'=64,'dp'=2] {'expert','dp'}, dimensions={0} | all-to-all | bytes 8388608 | tf_op jit(solution)/shard_map/all_to_all | solution.py:60
  74.7 0.0 copy-start.6
  74.7 1.8 %slice.9 = bf16[128,4,3584]{2,1,0:T(4,128)(2,1)S(1)} slice(bf16[128,4,4096]{2,1,0:T(4,128)(2,1)S(1)} %all_to_all.10), slice={[0:128], [0:4], [0:3584]} | slice | bytes 7340032 | tf_op jit(solution)/shard_map/slice | solution.py:61
  76.5 0.0 copy-start.2
  76.5 0.3 slice.8
  76.8 0.0 copy-done.6
  76.8 0.0 copy-start.5
  76.8 2.2 %fusion.37 = (bf16[128,4,512]{2,0,1:T(8,128)(2,1)S(1)}, f32[128,4,512]{2,0,1:T(8,128)S(1)}) fusion(bf16[128,4,512]{2,1,0:T(4,128)(2,1)S(1)} %slice.8, bf16[1,3584,512]{2,1,0:T(8,128)(2,1)S(1)} %copy-done.6, bf16[128,4,3584]{2,1,0:T(4,128)(2,1)S(1)} %slice.9), kind=kOutput, calls=%fused_computation.29 | convolution fusion | flops 1880883200 | bytes 9437184 | tf_op jit(solution)/shard_map/skd,df->skf/dot_general | solution.py:8
  79.0 0.0 copy-done.2
  79.0 0.8 copy-done.5
  79.8 2.3 %fusion.31 = bf16[128,4,512]{2,0,1:T(8,128)(2,1)S(1)} fusion(bf16[1,3584,512]{2,1,0:T(8,128)(2,1)S(1)} %copy-done.5, bf16[128,4,3584]{2,1,0:T(4,128)(2,1)S(1)} %slice.9, f32[128,4,512]{2,0,1:T(8,128)S(1)} %get-tuple-element.4, bf16[128,4,512]{2,1,0:T(4,128)(2,1)S(1)} %slice.8), kind=kOutput, calls=%fused_computation.26 | convolution fusion | flops 1881931776 | bytes 9437184 | tf_op jit(solution)/shard_map/skd,df->skf/dot_general | solution.py:9
  82.2 4.3 %fusion.3 = bf16[128,4,3584]{2,0,1:T(8,128)(2,1)S(1)} fusion(bf16[3584,512]{1,0:T(8,128)(2,1)S(1)} %bitcast.52, bf16[3584,512]{1,0:T(8,128)(2,1)S(1)} %bitcast.53, bf16[128,4,512]{2,0,1:T(8,128)(2,1)S(1)} %get-tuple-element.3, bf16[128,4,512]{2,0,1:T(8,128)(2,1)S(1)} %fusion.31), kind=kOutput, calls=%fused_computation.6 | convolution fusion | flops 3776708608 | bytes 12058624 | tf_op jit(solution)/shard_map/skf,df->skd/dot_general | solution.py:16
  86.4 4.7 %copy.28 = bf16[128,4,3584]{2,1,0:T(4,128)(2,1)} copy(bf16[128,4,3584]{2,0,1:T(8,128)(2,1)S(1)} %fusion.3) | data formatting | bytes 7340032 | tf_op jit(solution)/shard_map/convert_element_type | solution.py:24
  91.1 5.6 %all-to-all-start.1 = ((bf16[128,4,3584]{2,1,0:T(4,128)(2,1)}), bf16[128,4,3584]{2,1,0:T(4,128)(2,1)}, u32[]{:S(2)}, u32[]{:S(2)}) async-start(bf16[128,4,3584]{2,1,0:T(4,128)(2,1)} %copy.28), calls=%async_computation.1 | async-start | bytes 7340032 | tf_op jit(solution)/shard_map/all_to_all | solution.py:66
  96.7 0.1 compare_convert_fusion
  96.8 0.0 copy-start.3
  96.8 6.1 %fusion.4 = bf16[1,3584,512]{2,1,0:T(8,128)(2,1)} fusion(bf16[128,4,512]{2,0,1:T(8,128)(2,1)S(1)} %fusion.31, bf16[128,4,3584]{2,1,0:T(4,128)(2,1)} %copy-done.2), kind=kOutput, calls=%fused_computation.7 | convolution fusion | flops 1880883200 | bytes 7864320 | tf_op jit(solution)/shard_map/skd,skf->df/dot_general | solution.py:22
  103.0 0.0 copy-done.3
  103.0 3.9 %fusion.5 = bf16[1,3584,512]{2,1,0:T(8,128)(2,1)} fusion(bf16[128,4,512]{2,0,1:T(8,128)(2,1)S(1)} %get-tuple-element.3, bf16[128,4,3584]{2,1,0:T(4,128)(2,1)S(1)} %copy-done.3), kind=kOutput, calls=%fused_computation.8 | convolution fusion | flops 1880883200 | bytes 7864320 | tf_op jit(solution)/shard_map/skd,skf->df/dot_general | solution.py:23
  106.9 36.8 %all-to-all-done.1 = bf16[128,4,3584]{2,1,0:T(4,128)(2,1)} async-done(((bf16[128,4,3584]{2,1,0:T(4,128)(2,1)}), bf16[128,4,3584]{2,1,0:T(4,128)(2,1)}, u32[]{:S(2)}, u32[]{:S(2)}) %all-to-all-start.1) | async-done | bytes 3670048 | tf_op jit(solution)/shard_map/all_to_all | solution.py:66
  143.7 0.1 broadcast_in_dim.10
  143.8 3.9 %fusion.6 = bf16[128,3584]{1,0:T(8,128)(2,1)} fusion(bf16[128,4,128]{2,0,1:T(8,128)(2,1)S(1)} %bitcast.51, bf16[128,4,3584]{2,1,0:T(4,128)(2,1)} %all-to-all-done.1), kind=kOutput, calls=%fused_computation.11 | convolution fusion | flops 470220800 | bytes 4718592 | tf_op jit(solution)/shard_map/dot_general | solution.py:70
  (1 shorter events, 0.0 us)
Async XLA Ops:
  0.6 1.6 %copy-start = (bf16[128,3584]{1,0:T(8,128)(2,1)S(1)}, bf16[128,3584]{1,0:T(8,128)(2,1)}, u32[]{:S(2)}) copy-start(bf16[128,3584]{1,0:T(8,128)(2,1)} %param.5) | copy-start | bytes 2752516
  0.6 3.7 %copy-start.4 = (bf16[128,1024]{1,0:T(8,128)(2,1)S(1)}, bf16[128,1024]{1,0:T(8,128)(2,1)}, u32[]{:S(2)}) copy-start(bf16[128,1024]{1,0:T(8,128)(2,1)} %param.6) | copy-start | bytes 786436
  4.3 2.7 %copy-start.1 = (bf16[64,4,3584]{2,1,0:T(4,128)(2,1)S(1)}, bf16[64,4,3584]{2,1,0:T(4,128)(2,1)}, u32[]{:S(2)}) copy-start(bf16[64,4,3584]{2,1,0:T(4,128)(2,1)} %broadcast_in_dim.11) | copy-start | bytes 5505028
  74.7 2.1 %copy-start.6 = (bf16[1,3584,512]{2,1,0:T(8,128)(2,1)S(1)}, bf16[1,3584,512]{2,1,0:T(8,128)(2,1)}, u32[]{:S(2)}) copy-start(bf16[1,3584,512]{2,1,0:T(8,128)(2,1)} %param.8) | copy-start | bytes 11010052
  76.5 2.6 %copy-start.2 = (bf16[128,4,3584]{2,1,0:T(4,128)(2,1)}, bf16[128,4,3584]{2,1,0:T(4,128)(2,1)S(1)}, u32[]{:S(2)}) copy-start(bf16[128,4,3584]{2,1,0:T(4,128)(2,1)S(1)} %slice.9) | copy-start | bytes 11010052
  76.8 3.1 %copy-start.5 = (bf16[1,3584,512]{2,1,0:T(8,128)(2,1)S(1)}, bf16[1,3584,512]{2,1,0:T(8,128)(2,1)}, u32[]{:S(2)}) copy-start(bf16[1,3584,512]{2,1,0:T(8,128)(2,1)} %param.9) | copy-start | bytes 11010052
  91.1 52.6 %all-to-all-start.1 = ((bf16[128,4,3584]{2,1,0:T(4,128)(2,1)}), bf16[128,4,3584]{2,1,0:T(4,128)(2,1)}, u32[]{:S(2)}, u32[]{:S(2)}) async-start(bf16[128,4,3584]{2,1,0:T(4,128)(2,1)} %copy.28), calls=%async_computation.1 | async-start | bytes 7340032 | tf_op jit(solution)/shard_map/all_to_all | solution.py:66
  96.8 6.2 %copy-start.3 = (bf16[128,4,3584]{2,1,0:T(4,128)(2,1)S(1)}, bf16[128,4,3584]{2,1,0:T(4,128)(2,1)}, u32[]{:S(2)}) copy-start(bf16[128,4,3584]{2,1,0:T(4,128)(2,1)} %copy-done.2) | copy-start | bytes 11010052

commit v7 on v6

--- a/solution.py
+++ b/solution.py
@@ -44,11 +44,20 @@
         jnp.bfloat16
     )
     send_rows = jnp.dot(pick, tokens, preferred_element_type=jnp.float32).astype(jnp.bfloat16)
-    send_cot = jnp.dot(pick, cotangent, preferred_element_type=jnp.float32).astype(jnp.bfloat16)
+    send_cot = jnp.stack(
+        [
+            jnp.dot(
+                pick,
+                cotangent[:, copy * half_width : (copy + 1) * half_width],
+                preferred_element_type=jnp.float32,
+            )
+            .astype(jnp.bfloat16)
+            .reshape(n_experts, most_rows, half_width)
+            for copy in range(n_dp)
+        ],
+        axis=1,
+    )
     send_rows = send_rows.reshape(n_experts, 1, most_rows, model_width)
-    send_cot = jnp.swapaxes(
-        send_cot.reshape(n_experts, most_rows, n_dp, half_width), 1, 2
-    )
     packed = jnp.concatenate(
         [
             jnp.broadcast_to(send_rows, (n_experts, n_dp, most_rows, model_width)),

time: 148 us -> 150 us (1.014)
    broadcast_in_dim x2, local copies, waits for them, and re-layouts: 2.4 us -> 3.9 us  [per_device(): jnp.broadcast_to(send_rows, (n_experts, n_dp, most_rows, model_width))]
where the time goes in v7:
time: 150 us; the launch traced here: 149 us
  blocking collectives  64 us (43%)
  waiting for transfers between devices  36.8 us (25%)
  matrix products  25.6 us (17%)
  local copies, waits for them, and re-layouts  12.2 us (8%)
  starting transfers between devices  5.62 us (4%)
  other arithmetic  4.25 us (3%)
    all_to_all x1, blocking collectives, per_device(): lax.all_to_all(packed, ('expert', 'dp'), split_axis=0, concat_axis=0, til...  64 us
    all_to_all x1, waiting for transfers between devices, per_device(): lax.all_to_all(back, ('expert', 'dp'), split_axis=0, concat_axis=0, tiled...  36.8 us
    dot_general x1, matrix products, expert_math(): jnp.einsum('skd,skf->df', rows, d_gate, preferred_element_type=jnp.float32)  6.14 us
    all_to_all x1, starting transfers between devices, per_device(): lax.all_to_all(back, ('expert', 'dp'), split_axis=0, concat_axis=0, tiled...  5.62 us
    convert_element_type x1, local copies, waits for them, and re-layouts, expert_math(): back.astype(jnp.bfloat16)  4.67 us
    dot_general x1, matrix products, expert_math(): jnp.einsum('skf,df->skd', jnp.concatenate([d_gate, d_up], axis=2), jnp.co...  4.23 us
    dot_general x1, matrix products, expert_math(): jnp.einsum('skd,skf->df', rows, d_up, preferred_element_type=jnp.float32)  3.94 us
    broadcast_in_dim x2, local copies, waits for them, and re-layouts, per_device(): jnp.broadcast_to(send_rows, (n_experts, n_dp, most_rows, model_width))  3.9 us
  transfers between devices with their start and end apart: 1, of which 1 were waited for; matrix products, arithmetic and copies ran while one was open for 7% of the time, Pallas kernels for 0%

profile of v7, /device:TPU:1, one launch (start us, length us, event | category | flops | bytes accessed | tf_op | source)
XLA Modules:
  0.0 149.2 jit_solution(17856058592571483590)
XLA Ops:
  0.6 0.0 copy-start
  0.6 0.9 convert_reduce_fusion
  1.6 0.7 multiply_add_fusion.1
  2.2 1.1 convolution_convert_fusion.1
  3.4 1.1 convolution_convert_fusion.2
  4.5 0.0 copy-done
  4.5 0.6 convolution_convert_fusion
  5.1 1.5 broadcast_in_dim.11
  6.6 0.1 stack_reshape.7
  6.6 0.1 stack_reshape.6
  6.7 2.4 %broadcast_in_dim.24 = bf16[64,2,4,3584]{3,2,1,0:T(4,128)(2,1)S(1)} broadcast(bf16[64,4,3584]{2,1,0:T(4,128)(2,1)} %broadcast_in_dim.11), dimensions={0,2,3} | broadcast | bytes 5505024 | tf_op jit(solution)/shard_map/broadcast_in_dim | solution.py:63
  9.2 2.6 %pad_maximum_fusion = bf16[64,2,4,4096]{3,2,1,0:T(4,128)(2,1)S(1)} fusion(bf16[64,2,4,3584]{3,2,1,0:T(4,128)(2,1)S(1)} %broadcast_in_dim.24, bf16[64,1,4,512]{3,2,0,1:T(4,128)(2,1)S(1)} %stack_reshape.7, bf16[64,1,4,512]{3,2,0,1:T(4,128)(2,1)S(1)} %stack_reshape.6), kind=kLoop, calls=%fused_computation.12 | loop fusion | flops 8650752 | bytes 8388608 | tf_op jit(solution)/shard_map/concatenate | solution.py:61
  11.7 64.0 %all_to_all.10 = bf16[128,4,4096]{2,1,0:T(4,128)(2,1)S(1)} all-to-all(bf16[128,4,4096]{2,1,0:T(4,128)(2,1)S(1)} %bitcast.47), channel_id=1, replica_groups=mesh['expert'=64,'dp'=2] {'expert','dp'}, dimensions={0} | all-to-all | bytes 8388608 | tf_op jit(solution)/shard_map/all_to_all | solution.py:69
  75.7 0.3 slice.16
  76.0 0.0 copy-start.4
  76.0 1.8 %slice.17 = bf16[128,4,3584]{2,1,0:T(4,128)(2,1)S(1)} slice(bf16[128,4,4096]{2,1,0:T(4,128)(2,1)S(1)} %all_to_all.10), slice={[0:128], [0:4], [0:3584]} | slice | bytes 7340032 | tf_op jit(solution)/shard_map/slice | solution.py:70
  77.8 0.2 copy-done.4
  78.1 0.0 copy-start.1
  78.1 0.0 copy-start.3
  78.1 2.2 %fusion.37 = (bf16[128,4,512]{2,0,1:T(8,128)(2,1)S(1)}, f32[128,4,512]{2,0,1:T(8,128)S(1)}) fusion(bf16[128,4,512]{2,1,0:T(4,128)(2,1)S(1)} %slice.16, bf16[1,3584,512]{2,1,0:T(8,128)(2,1)S(1)} %copy-done.4, bf16[128,4,3584]{2,1,0:T(4,128)(2,1)S(1)} %slice.17), kind=kOutput, calls=%fused_computation.30 | convolution fusion | flops 1880883200 | bytes 9437184 | tf_op jit(solution)/shard_map/skd,df->skf/dot_general | solution.py:8
  80.3 0.0 copy-done.1
  80.3 1.1 copy-done.3
  81.4 2.3 %fusion.31 = bf16[128,4,512]{2,0,1:T(8,128)(2,1)S(1)} fusion(bf16[1,3584,512]{2,1,0:T(8,128)(2,1)S(1)} %copy-done.3, bf16[128,4,3584]{2,1,0:T(4,128)(2,1)S(1)} %slice.17, f32[128,4,512]{2,0,1:T(8,128)S(1)} %get-tuple-element.4, bf16[128,4,512]{2,1,0:T(4,128)(2,1)S(1)} %slice.16), kind=kOutput, calls=%fused_computation.26 | convolution fusion | flops 1881931776 | bytes 9437184 | tf_op jit(solution)/shard_map/skd,df->skf/dot_general | solution.py:9
  83.7 4.2 %fusion.3 = bf16[128,4,3584]{2,0,1:T(8,128)(2,1)S(1)} fusion(bf16[3584,512]{1,0:T(8,128)(2,1)S(1)} %bitcast.49, bf16[3584,512]{1,0:T(8,128)(2,1)S(1)} %bitcast.50, bf16[128,4,512]{2,0,1:T(8,128)(2,1)S(1)} %get-tuple-element.3, bf16[128,4,512]{2,0,1:T(8,128)(2,1)S(1)} %fusion.31), kind=kOutput, calls=%fused_computation.6 | convolution fusion | flops 3776708608 | bytes 12058624 | tf_op jit(solution)/shard_map/skf,df->skd/dot_general | solution.py:16
  88.0 4.7 %copy.28 = bf16[128,4,3584]{2,1,0:T(4,128)(2,1)} copy(bf16[128,4,3584]{2,0,1:T(8,128)(2,1)S(1)} %fusion.3) | data formatting | bytes 7340032 | tf_op jit(solution)/shard_map/convert_element_type | solution.py:24
  92.6 5.6 %all-to-all-start.1 = ((bf16[128,4,3584]{2,1,0:T(4,128)(2,1)}), bf16[128,4,3584]{2,1,0:T(4,128)(2,1)}, u32[]{:S(2)}, u32[]{:S(2)}) async-start(bf16[128,4,3584]{2,1,0:T(4,128)(2,1)} %copy.28), calls=%async_computation.1 | async-start | bytes 7340032 | tf_op jit(solution)/shard_map/all_to_all | solution.py:75
  98.3 0.1 compare_convert_fusion
  98.4 0.0 copy-start.2
  98.4 6.1 %fusion.4 = bf16[1,3584,512]{2,1,0:T(8,128)(2,1)} fusion(bf16[128,4,512]{2,0,1:T(8,128)(2,1)S(1)} %fusion.31, bf16[128,4,3584]{2,1,0:T(4,128)(2,1)} %copy-done.1), kind=kOutput, calls=%fused_computation.7 | convolution fusion | flops 1880883200 | bytes 7864320 | tf_op jit(solution)/shard_map/skd,skf->df/dot_general | solution.py:22
  104.5 0.0 copy-done.2
  104.5 3.9 %fusion.5 = bf16[1,3584,512]{2,1,0:T(8,128)(2,1)} fusion(bf16[128,4,512]{2,0,1:T(8,128)(2,1)S(1)} %get-tuple-element.3, bf16[128,4,3584]{2,1,0:T(4,128)(2,1)S(1)} %copy-done.2), kind=kOutput, calls=%fused_computation.8 | convolution fusion | flops 1880883200 | bytes 7864320 | tf_op jit(solution)/shard_map/skd,skf->df/dot_general | solution.py:23
  108.5 36.8 %all-to-all-done.1 = bf16[128,4,3584]{2,1,0:T(4,128)(2,1)} async-done(((bf16[128,4,3584]{2,1,0:T(4,128)(2,1)}), bf16[128,4,3584]{2,1,0:T(4,128)(2,1)}, u32[]{:S(2)}, u32[]{:S(2)}) %all-to-all-start.1) | async-done | bytes 3670048 | tf_op jit(solution)/shard_map/all_to_all | solution.py:75
  145.3 0.1 broadcast_in_dim.10
  145.3 3.9 %fusion.6 = bf16[128,3584]{1,0:T(8,128)(2,1)} fusion(bf16[128,4,128]{2,0,1:T(8,128)(2,1)S(1)} %bitcast.48, bf16[128,4,3584]{2,1,0:T(4,128)(2,1)} %all-to-all-done.1), kind=kOutput, calls=%fused_computation.11 | convolution fusion | flops 470220800 | bytes 4718592 | tf_op jit(solution)/shard_map/dot_general | solution.py:79
  (1 shorter events, 0.0 us)
Async XLA Ops:
  0.6 3.9 %copy-start = (bf16[128,3584]{1,0:T(8,128)(2,1)S(1)}, bf16[128,3584]{1,0:T(8,128)(2,1)}, u32[]{:S(2)}) copy-start(bf16[128,3584]{1,0:T(8,128)(2,1)} %param.5) | copy-start | bytes 2752516
  76.0 2.0 %copy-start.4 = (bf16[1,3584,512]{2,1,0:T(8,128)(2,1)S(1)}, bf16[1,3584,512]{2,1,0:T(8,128)(2,1)}, u32[]{:S(2)}) copy-start(bf16[1,3584,512]{2,1,0:T(8,128)(2,1)} %param.8) | copy-start | bytes 11010052
  78.1 2.3 %copy-start.1 = (bf16[128,4,3584]{2,1,0:T(4,128)(2,1)}, bf16[128,4,3584]{2,1,0:T(4,128)(2,1)S(1)}, u32[]{:S(2)}) copy-start(bf16[128,4,3584]{2,1,0:T(4,128)(2,1)S(1)} %slice.17) | copy-start | bytes 11010052
  78.1 3.4 %copy-start.3 = (bf16[1,3584,512]{2,1,0:T(8,128)(2,1)S(1)}, bf16[1,3584,512]{2,1,0:T(8,128)(2,1)}, u32[]{:S(2)}) copy-start(bf16[1,3584,512]{2,1,0:T(8,128)(2,1)} %param.9) | copy-start | bytes 11010052
  92.6 52.6 %all-to-all-start.1 = ((bf16[128,4,3584]{2,1,0:T(4,128)(2,1)}), bf16[128,4,3584]{2,1,0:T(4,128)(2,1)}, u32[]{:S(2)}, u32[]{:S(2)}) async-start(bf16[128,4,3584]{2,1,0:T(4,128)(2,1)} %copy.28), calls=%async_computation.1 | async-start | bytes 7340032 | tf_op jit(solution)/shard_map/all_to_all | solution.py:75
  98.4 6.2 %copy-start.2 = (bf16[128,4,3584]{2,1,0:T(4,128)(2,1)S(1)}, bf16[128,4,3584]{2,1,0:T(4,128)(2,1)}, u32[]{:S(2)}) copy-start(bf16[128,4,3584]{2,1,0:T(4,128)(2,1)} %copy-done.1) | copy-start | bytes 11010052

commit v8 on v6

--- a/solution.py
+++ b/solution.py
@@ -21,7 +21,7 @@
     )
     grad_g = jnp.einsum("skd,skf->df", rows, d_gate, preferred_element_type=jnp.float32)
     grad_u = jnp.einsum("skd,skf->df", rows, d_up, preferred_element_type=jnp.float32)
-    return back.astype(jnp.bfloat16), grad_g.astype(jnp.bfloat16), grad_u.astype(jnp.bfloat16)
+    return back, grad_g.astype(jnp.bfloat16), grad_u.astype(jnp.bfloat16)
 
 
 def per_device(tokens, cotangent, routing, w_gate, w_up):
@@ -68,7 +68,11 @@
         pick.reshape(n_experts, 1, most_rows, tok_rows), (n_experts, n_dp, most_rows, tok_rows)
     ).reshape(n_experts * n_dp, most_rows, tok_rows)
     grad_tokens = lax.dot_general(
-        pick_dup, returned, (((0, 1), (0, 1)), ((), ())), preferred_element_type=jnp.float32
+        pick_dup.astype(jnp.float32),
+        returned,
+        (((0, 1), (0, 1)), ((), ())),
+        precision=lax.Precision.HIGHEST,
+        preferred_element_type=jnp.float32,
     ).astype(jnp.bfloat16)
     return grad_tokens, grad_g[None], grad_u[None]
 

time: 148 us -> 199 us (1.34)
  waiting for transfers between devices: 36.8 us -> 78.9 us
  matrix products: 24.5 us -> 28.9 us
  local copies, waits for them, and re-layouts: 11.7 us -> 15.8 us
    all_to_all x1, waiting for transfers between devices: 36.8 us -> 78.9 us  [per_device(): lax.all_to_all(back, ('expert', 'dp'), split_axis=0, concat_axis=0, tiled...]
    dot_general x0 -> x1, local copies, waits for them, and re-layouts: none -> 7.95 us  [expert_math(): jnp.einsum('skf,df->skd', jnp.concatenate([d_gate, d_up], axis=2), jnp.co...]
    dot_general x1, matrix products: 3.89 us -> 8.58 us  [per_device(): lax.dot_general(pick_dup.astype(jnp.float32), returned, (((0, 1), (0, 1))...]
    convert_element_type x1 -> x0, local copies, waits for them, and re-layouts: 4.66 us -> none  [expert_math(): back.astype(jnp.bfloat16)]
  transfers between devices with their start and end apart: 1 -> 1, of which waited for: 1 -> 1; matrix products, arithmetic and copies ran while one was open for 7% -> 5% of each run, Pallas kernels for 0% -> 0%
where the time goes in v8:
time: 199 us
  waiting for transfers between devices  78.9 us (40%)
  blocking collectives  64 us (32%)
  matrix products  28.9 us (15%)
  local copies, waits for them, and re-layouts  15.8 us (8%)
  starting transfers between devices  5.81 us (3%)
  other arithmetic  4.31 us (2%)
    all_to_all x1, waiting for transfers between devices, per_device(): lax.all_to_all(back, ('expert', 'dp'), split_axis=0, concat_axis=0, tiled...  78.9 us
    all_to_all x1, blocking collectives, per_device(): lax.all_to_all(packed, ('expert', 'dp'), split_axis=0, concat_axis=0, til...  64 us
    dot_general x1, matrix products, per_device(): lax.dot_general(pick_dup.astype(jnp.float32), returned, (((0, 1), (0, 1))...  8.58 us
    dot_general x1, local copies, waits for them, and re-layouts, expert_math(): jnp.einsum('skf,df->skd', jnp.concatenate([d_gate, d_up], axis=2), jnp.co...  7.95 us
    dot_general x1, matrix products, expert_math(): jnp.einsum('skd,skf->df', rows, d_gate, preferred_element_type=jnp.float32)  6.14 us
    all_to_all x1, starting transfers between devices, per_device(): lax.all_to_all(back, ('expert', 'dp'), split_axis=0, concat_axis=0, tiled...  5.81 us
    dot_general x1, matrix products, expert_math(): jnp.einsum('skf,df->skd', jnp.concatenate([d_gate, d_up], axis=2), jnp.co...  3.98 us
  transfers between devices with their start and end apart: 1, of which 1 were waited for; matrix products, arithmetic and copies ran while one was open for 5% of the time, Pallas kernels for 0%

profile of v8, /device:TPU:1, one launch (start us, length us, event | category | flops | bytes accessed | tf_op | source)
XLA Modules:
  0.0 198.5 jit_solution(14985585791659770096)
XLA Ops:
  0.6 0.0 copy-start
  0.6 0.0 copy-start.4
  0.7 0.9 convert_reduce_fusion
  1.6 0.7 multiply_add_fusion.1
  2.3 0.0 copy-done
  2.3 0.6 convolution_convert_fusion
  2.9 1.5 broadcast_in_dim.11
  4.3 0.0 copy-done.4
  4.3 0.0 copy-start.1
  4.3 1.1 convolution_convert_fusion.1
  5.4 1.4 reshape.43
  6.9 0.2 copy.25
  7.1 0.0 copy-done.1
  7.1 0.9 broadcast_in_dim.24
  8.0 2.6 %pad_maximum_fusion = bf16[64,2,4,4096]{3,2,1,0:T(4,128)(2,1)S(1)} fusion(bf16[64,2,4,512]{3,2,1,0:T(4,128)(2,1)S(1)} %copy.25, bf16[64,2,4,3584]{3,2,1,0:T(4,128)(2,1)S(1)} %broadcast_in_dim.24), kind=kLoop, calls=%fused_computation.13 | loop fusion | flops 8388608 | bytes 8388608 | tf_op jit(solution)/shard_map/concatenate | solution.py:52
  10.7 64.0 %all_to_all.10 = bf16[128,4,4096]{2,1,0:T(4,128)(2,1)S(1)} all-to-all(bf16[128,4,4096]{2,1,0:T(4,128)(2,1)S(1)} %bitcast.47), channel_id=1, replica_groups=mesh['expert'=64,'dp'=2] {'expert','dp'}, dimensions={0} | all-to-all | bytes 8388608 | tf_op jit(solution)/shard_map/all_to_all | solution.py:60
  74.7 0.0 copy-start.6
  74.7 1.8 slice.9
  76.5 0.0 copy-start.2
  76.5 0.3 slice.8
  76.8 0.0 copy-done.6
  76.8 0.0 copy-start.5
  76.8 2.2 %fusion.42 = (bf16[128,4,512]{2,0,1:T(8,128)(2,1)S(1)}, f32[128,4,512]{2,0,1:T(8,128)S(1)}) fusion(bf16[128,4,512]{2,1,0:T(4,128)(2,1)S(1)} %slice.8, bf16[1,3584,512]{2,1,0:T(8,128)(2,1)S(1)} %copy-done.6, bf16[128,4,3584]{2,1,0:T(4,128)(2,1)S(1)} %slice.9), kind=kOutput, calls=%fused_computation.29 | convolution fusion | flops 1880883200 | bytes 9437184 | tf_op jit(solution)/shard_map/skd,df->skf/dot_general | solution.py:8
  79.0 0.0 copy-done.2
  79.0 0.8 copy-done.5
  79.8 2.3 %fusion.36 = bf16[128,4,512]{2,0,1:T(8,128)(2,1)S(1)} fusion(bf16[1,3584,512]{2,1,0:T(8,128)(2,1)S(1)} %copy-done.5, bf16[128,4,3584]{2,1,0:T(4,128)(2,1)S(1)} %slice.9, f32[128,4,512]{2,0,1:T(8,128)S(1)} %get-tuple-element.4, bf16[128,4,512]{2,1,0:T(4,128)(2,1)S(1)} %slice.8), kind=kOutput, calls=%fused_computation.26 | convolution fusion | flops 1881931776 | bytes 9437184 | tf_op jit(solution)/shard_map/skd,df->skf/dot_general | solution.py:9
  82.2 0.0 copy-start.7
  82.2 0.8 copy-done.7
  83.0 4.0 %fusion = f32[128,4,3584]{2,0,1:T(8,128)S(1)} fusion(bf16[3584,512]{1,0:T(8,128)(2,1)S(1)} %bitcast.50, bf16[3584,512]{1,0:T(8,128)(2,1)S(1)} %bitcast.51, bf16[128,4,512]{2,0,1:T(8,128)(2,1)S(1)} %get-tuple-element.3, bf16[128,4,512]{2,0,1:T(8,128)(2,1)S(1)} %fusion.36), kind=kOutput, calls=%fused_computation.1 | convolution fusion | flops 3774873600 | bytes 15728640 | tf_op jit(solution)/shard_map/skf,df->skd/dot_general | solution.py:16
  86.9 8.0 %copy.28 = f32[128,4,3584]{2,1,0:T(4,128)} copy(f32[128,4,3584]{2,0,1:T(8,128)S(1)} %fusion) | data formatting | bytes 14680064 | tf_op jit(solution)/shard_map/skf,df->skd/dot_general | solution.py:16
  94.9 0.0 copy-start.8
  94.9 5.8 %all-to-all-start.1 = ((f32[128,4,3584]{2,1,0:T(4,128)}), f32[128,4,3584]{2,1,0:T(4,128)}, u32[]{:S(2)}, u32[]{:S(2)}) async-start(f32[128,4,3584]{2,1,0:T(4,128)} %copy.28), calls=%async_computation.1 | async-start | bytes 14680064 | tf_op jit(solution)/shard_map/all_to_all | solution.py:66
  100.7 0.1 compare_convert_fusion
  100.8 0.0 copy-done.8
  100.8 0.0 copy-start.3
  100.9 6.1 %fusion.5 = bf16[1,3584,512]{2,1,0:T(8,128)(2,1)} fusion(bf16[128,4,512]{2,0,1:T(8,128)(2,1)S(1)} %copy-done.8, bf16[128,4,3584]{2,1,0:T(4,128)(2,1)} %copy-done.2), kind=kOutput, calls=%fused_computation.8 | convolution fusion | flops 1880883200 | bytes 7864320 | tf_op jit(solution)/shard_map/skd,skf->df/dot_general | solution.py:22
  107.0 0.0 copy-done.3
  107.0 3.9 %fusion.6 = bf16[1,3584,512]{2,1,0:T(8,128)(2,1)} fusion(bf16[128,4,512]{2,0,1:T(8,128)(2,1)S(1)} %get-tuple-element.3, bf16[128,4,3584]{2,1,0:T(4,128)(2,1)S(1)} %copy-done.3), kind=kOutput, calls=%fused_computation.9 | convolution fusion | flops 1880883200 | bytes 7864320 | tf_op jit(solution)/shard_map/skd,skf->df/dot_general | solution.py:23
  111.0 78.9 %all-to-all-done.1 = f32[128,4,3584]{2,1,0:T(4,128)} async-done(((f32[128,4,3584]{2,1,0:T(4,128)}), f32[128,4,3584]{2,1,0:T(4,128)}, u32[]{:S(2)}, u32[]{:S(2)}) %all-to-all-start.1) | async-done | bytes 7340064 | tf_op jit(solution)/shard_map/all_to_all | solution.py:66
  189.9 0.1 broadcast_in_dim.10
  189.9 8.6 %fusion.10 = bf16[128,3584]{1,0:T(8,128)(2,1)} fusion(bf16[128,4,128]{2,0,1:T(8,128)(2,1)S(1)} %bitcast.49, f32[128,4,3584]{2,1,0:T(4,128)} %all-to-all-done.1), kind=kOutput, calls=%fused_computation.12 | convolution fusion | flops 2819031040 | bytes 8388608 | tf_op jit(solution)/shard_map/dot_general | solution.py:70
  (1 shorter events, 0.0 us)
Async XLA Ops:
  0.6 1.6 copy-start
  0.6 3.7 %copy-start.4 = (bf16[128,1024]{1,0:T(8,128)(2,1)S(1)}, bf16[128,1024]{1,0:T(8,128)(2,1)}, u32[]{:S(2)}) copy-start(bf16[128,1024]{1,0:T(8,128)(2,1)} %param.6) | copy-start | bytes 786436
  4.3 2.7 %copy-start.1 = (bf16[64,4,3584]{2,1,0:T(4,128)(2,1)S(1)}, bf16[64,4,3584]{2,1,0:T(4,128)(2,1)}, u32[]{:S(2)}) copy-start(bf16[64,4,3584]{2,1,0:T(4,128)(2,1)} %broadcast_in_dim.11) | copy-start | bytes 5505028
  74.7 2.1 %copy-start.6 = (bf16[1,3584,512]{2,1,0:T(8,128)(2,1)S(1)}, bf16[1,3584,512]{2,1,0:T(8,128)(2,1)}, u32[]{:S(2)}) copy-start(bf16[1,3584,512]{2,1,0:T(8,128)(2,1)} %param.8) | copy-start | bytes 11010052
  76.5 2.6 %copy-start.2 = (bf16[128,4,3584]{2,1,0:T(4,128)(2,1)}, bf16[128,4,3584]{2,1,0:T(4,128)(2,1)S(1)}, u32[]{:S(2)}) copy-start(bf16[128,4,3584]{2,1,0:T(4,128)(2,1)S(1)} %slice.9) | copy-start | bytes 11010052
  76.8 3.1 %copy-start.5 = (bf16[1,3584,512]{2,1,0:T(8,128)(2,1)S(1)}, bf16[1,3584,512]{2,1,0:T(8,128)(2,1)}, u32[]{:S(2)}) copy-start(bf16[1,3584,512]{2,1,0:T(8,128)(2,1)} %param.9) | copy-start | bytes 11010052
  82.2 0.8 copy-start.7
  94.9 5.9 %copy-start.8 = (bf16[128,4,512]{2,0,1:T(8,128)(2,1)S(1)}, bf16[128,4,512]{2,0,1:T(8,128)(2,1)}, u32[]{:S(2)}) copy-start(bf16[128,4,512]{2,0,1:T(8,128)(2,1)} %copy-done.7) | copy-start | bytes 1572868
  94.9 95.0 %all-to-all-start.1 = ((f32[128,4,3584]{2,1,0:T(4,128)}), f32[128,4,3584]{2,1,0:T(4,128)}, u32[]{:S(2)}, u32[]{:S(2)}) async-start(f32[128,4,3584]{2,1,0:T(4,128)} %copy.28), calls=%async_computation.1 | async-start | bytes 14680064 | tf_op jit(solution)/shard_map/all_to_all | solution.py:66
  100.8 6.2 %copy-start.3 = (bf16[128,4,3584]{2,1,0:T(4,128)(2,1)S(1)}, bf16[128,4,3584]{2,1,0:T(4,128)(2,1)}, u32[]{:S(2)}) copy-start(bf16[128,4,3584]{2,1,0:T(4,128)(2,1)} %copy-done.2) | copy-start | bytes 11010052

commit v9 on v6

--- a/solution.py
+++ b/solution.py
@@ -43,8 +43,11 @@
     pick = (jnp.arange(slot_total, dtype=jnp.int32)[:, None] == dest[None, :]).astype(
         jnp.bfloat16
     )
-    send_rows = jnp.dot(pick, tokens, preferred_element_type=jnp.float32).astype(jnp.bfloat16)
-    send_cot = jnp.dot(pick, cotangent, preferred_element_type=jnp.float32).astype(jnp.bfloat16)
+    send_both = jnp.dot(
+        pick, jnp.concatenate([tokens, cotangent], axis=1), preferred_element_type=jnp.float32
+    ).astype(jnp.bfloat16)
+    send_rows = send_both[:, :model_width]
+    send_cot = send_both[:, model_width:]
     send_rows = send_rows.reshape(n_experts, 1, most_rows, model_width)
     send_cot = jnp.swapaxes(
         send_cot.reshape(n_experts, most_rows, n_dp, half_width), 1, 2

time: 148 us -> 149 us (level)
    broadcast_in_dim x2, local copies, waits for them, and re-layouts: 2.4 us -> 3.9 us  [per_device(): jnp.broadcast_to(send_rows, (n_experts, n_dp, most_rows, model_width))]
where the time goes in v9:
time: 149 us
  blocking collectives  64 us (43%)
  waiting for transfers between devices  36.8 us (25%)
  matrix products  24.8 us (17%)
  local copies, waits for them, and re-layouts  12.3 us (8%)
  starting transfers between devices  5.62 us (4%)
  other arithmetic  4.27 us (3%)
    all_to_all x1, blocking collectives, per_device(): lax.all_to_all(packed, ('expert', 'dp'), split_axis=0, concat_axis=0, til...  64 us
    all_to_all x1, waiting for transfers between devices, per_device(): lax.all_to_all(back, ('expert', 'dp'), split_axis=0, concat_axis=0, tiled...  36.8 us
    dot_general x1, matrix products, expert_math(): jnp.einsum('skd,skf->df', rows, d_gate, preferred_element_type=jnp.float32)  6.14 us
    all_to_all x1, starting transfers between devices, per_device(): lax.all_to_all(back, ('expert', 'dp'), split_axis=0, concat_axis=0, tiled...  5.62 us
    convert_element_type x1, local copies, waits for them, and re-layouts, expert_math(): back.astype(jnp.bfloat16)  4.68 us
    dot_general x1, matrix products, expert_math(): jnp.einsum('skf,df->skd', jnp.concatenate([d_gate, d_up], axis=2), jnp.co...  4.26 us
    dot_general x1, matrix products, expert_math(): jnp.einsum('skd,skf->df', rows, d_up, preferred_element_type=jnp.float32)  3.95 us
    broadcast_in_dim x2, local copies, waits for them, and re-layouts, per_device(): jnp.broadcast_to(send_rows, (n_experts, n_dp, most_rows, model_width))  3.9 us
  transfers between devices with their start and end apart: 1, of which 1 were waited for; matrix products, arithmetic and copies ran while one was open for 7% of the time, Pallas kernels for 0%

profile of v9, /device:TPU:1, one launch (start us, length us, event | category | flops | bytes accessed | tf_op | source)
XLA Modules:
  0.0 148.5 jit_solution(8746299474612672663)
XLA Ops:
  0.6 0.9 convert_reduce_fusion
  1.5 0.7 multiply_add_fusion.1
  2.2 2.0 %convolution_convert_fusion = bf16[256,4608]{1,0:T(8,128)(2,1)S(1)} fusion(bf16[128,1024]{1,0:T(8,128)(2,1)} %param.6, bf16[128,3584]{1,0:T(8,128)(2,1)} %param.5, s32[128]{0:T(128)S(1)} %multiply_add_fusion.1), kind=kOutput, calls=%fused_computation.6 | convolution fusion | flops 305561600 | bytes 3539456 | tf_op jit(solution)/shard_map/dot_general | solution.py:46
  4.2 0.1 slice.16
  4.4 0.1 slice.17
  4.4 1.5 broadcast_in_dim.11
  5.9 0.4 reshape.43
  6.2 0.2 copy.25
  6.5 2.4 %broadcast_in_dim.24 = bf16[64,2,4,3584]{3,2,1,0:T(4,128)(2,1)S(1)} broadcast(bf16[64,4,3584]{2,1,0:T(4,128)(2,1)} %broadcast_in_dim.11), dimensions={0,2,3} | broadcast | bytes 5505024 | tf_op jit(solution)/shard_map/broadcast_in_dim | solution.py:57
  8.9 2.6 %pad_maximum_fusion = bf16[64,2,4,4096]{3,2,1,0:T(4,128)(2,1)S(1)} fusion(bf16[64,2,4,512]{3,2,1,0:T(4,128)(2,1)S(1)} %copy.25, bf16[64,2,4,3584]{3,2,1,0:T(4,128)(2,1)S(1)} %broadcast_in_dim.24), kind=kLoop, calls=%fused_computation.12 | loop fusion | flops 8388608 | bytes 8388608 | tf_op jit(solution)/shard_map/concatenate | solution.py:55
  11.5 64.0 %all_to_all.10 = bf16[128,4,4096]{2,1,0:T(4,128)(2,1)S(1)} all-to-all(bf16[128,4,4096]{2,1,0:T(4,128)(2,1)S(1)} %bitcast.47), channel_id=1, replica_groups=mesh['expert'=64,'dp'=2] {'expert','dp'}, dimensions={0} | all-to-all | bytes 8388608 | tf_op jit(solution)/shard_map/all_to_all | solution.py:63
  75.5 0.0 copy-start.3
  75.5 1.8 %slice.19 = bf16[128,4,3584]{2,1,0:T(4,128)(2,1)S(1)} slice(bf16[128,4,4096]{2,1,0:T(4,128)(2,1)S(1)} %all_to_all.10), slice={[0:128], [0:4], [0:3584]} | slice | bytes 7340032 | tf_op jit(solution)/shard_map/slice | solution.py:64
  77.4 0.0 copy-start
  77.4 0.3 slice.18
  77.6 0.0 copy-done.3
  77.7 0.0 copy-start.2
  77.7 2.2 %fusion.40 = (bf16[128,4,512]{2,0,1:T(8,128)(2,1)S(1)}, f32[128,4,512]{2,0,1:T(8,128)S(1)}) fusion(bf16[128,4,512]{2,1,0:T(4,128)(2,1)S(1)} %slice.18, bf16[1,3584,512]{2,1,0:T(8,128)(2,1)S(1)} %copy-done.3, bf16[128,4,3584]{2,1,0:T(4,128)(2,1)S(1)} %slice.19), kind=kOutput, calls=%fused_computation.31 | convolution fusion | flops 1880883200 | bytes 9437184 | tf_op jit(solution)/shard_map/skd,df->skf/dot_general | solution.py:8
  79.9 0.0 copy-done
  79.9 0.8 copy-done.2
  80.7 2.3 %fusion.31 = bf16[128,4,512]{2,0,1:T(8,128)(2,1)S(1)} fusion(bf16[1,3584,512]{2,1,0:T(8,128)(2,1)S(1)} %copy-done.2, bf16[128,4,3584]{2,1,0:T(4,128)(2,1)S(1)} %slice.19, f32[128,4,512]{2,0,1:T(8,128)S(1)} %get-tuple-element.4, bf16[128,4,512]{2,1,0:T(4,128)(2,1)S(1)} %slice.18), kind=kOutput, calls=%fused_computation.26 | convolution fusion | flops 1881931776 | bytes 9437184 | tf_op jit(solution)/shard_map/skd,df->skf/dot_general | solution.py:9
  83.0 4.3 %fusion.3 = bf16[128,4,3584]{2,0,1:T(8,128)(2,1)S(1)} fusion(bf16[3584,512]{1,0:T(8,128)(2,1)S(1)} %bitcast.50, bf16[3584,512]{1,0:T(8,128)(2,1)S(1)} %bitcast.51, bf16[128,4,512]{2,0,1:T(8,128)(2,1)S(1)} %get-tuple-element.3, bf16[128,4,512]{2,0,1:T(8,128)(2,1)S(1)} %fusion.31), kind=kOutput, calls=%fused_computation.7 | convolution fusion | flops 3776708608 | bytes 12058624 | tf_op jit(solution)/shard_map/skf,df->skd/dot_general | solution.py:16
  87.3 4.7 %copy.28 = bf16[128,4,3584]{2,1,0:T(4,128)(2,1)} copy(bf16[128,4,3584]{2,0,1:T(8,128)(2,1)S(1)} %fusion.3) | data formatting | bytes 7340032 | tf_op jit(solution)/shard_map/convert_element_type | solution.py:24
  92.0 5.6 %all-to-all-start.1 = ((bf16[128,4,3584]{2,1,0:T(4,128)(2,1)}), bf16[128,4,3584]{2,1,0:T(4,128)(2,1)}, u32[]{:S(2)}, u32[]{:S(2)}) async-start(bf16[128,4,3584]{2,1,0:T(4,128)(2,1)} %copy.28), calls=%async_computation.1 | async-start | bytes 7340032 | tf_op jit(solution)/shard_map/all_to_all | solution.py:69
  97.6 0.1 compare_convert_fusion
  97.7 0.0 copy-start.1
  97.7 6.1 %fusion.4 = bf16[1,3584,512]{2,1,0:T(8,128)(2,1)} fusion(bf16[128,4,512]{2,0,1:T(8,128)(2,1)S(1)} %fusion.31, bf16[128,4,3584]{2,1,0:T(4,128)(2,1)} %copy-done), kind=kOutput, calls=%fused_computation.8 | convolution fusion | flops 1880883200 | bytes 7864320 | tf_op jit(solution)/shard_map/skd,skf->df/dot_general | solution.py:22
  103.9 0.0 copy-done.1
  103.9 3.9 %fusion.5 = bf16[1,3584,512]{2,1,0:T(8,128)(2,1)} fusion(bf16[128,4,512]{2,0,1:T(8,128)(2,1)S(1)} %get-tuple-element.3, bf16[128,4,3584]{2,1,0:T(4,128)(2,1)S(1)} %copy-done.1), kind=kOutput, calls=%fused_computation.9 | convolution fusion | flops 1880883200 | bytes 7864320 | tf_op jit(solution)/shard_map/skd,skf->df/dot_general | solution.py:23
  107.8 36.8 %all-to-all-done.1 = bf16[128,4,3584]{2,1,0:T(4,128)(2,1)} async-done(((bf16[128,4,3584]{2,1,0:T(4,128)(2,1)}), bf16[128,4,3584]{2,1,0:T(4,128)(2,1)}, u32[]{:S(2)}, u32[]{:S(2)}) %all-to-all-start.1) | async-done | bytes 3670048 | tf_op jit(solution)/shard_map/all_to_all | solution.py:69
  144.6 0.1 broadcast_in_dim.10
  144.7 3.9 %fusion.6 = bf16[128,3584]{1,0:T(8,128)(2,1)} fusion(bf16[128,4,128]{2,0,1:T(8,128)(2,1)S(1)} %bitcast.49, bf16[128,4,3584]{2,1,0:T(4,128)(2,1)} %all-to-all-done.1), kind=kOutput, calls=%fused_computation.11 | convolution fusion | flops 470220800 | bytes 4718592 | tf_op jit(solution)/shard_map/dot_general | solution.py:73
  (1 shorter events, 0.0 us)
Async XLA Ops:
  75.5 2.1 %copy-start.3 = (bf16[1,3584,512]{2,1,0:T(8,128)(2,1)S(1)}, bf16[1,3584,512]{2,1,0:T(8,128)(2,1)}, u32[]{:S(2)}) copy-start(bf16[1,3584,512]{2,1,0:T(8,128)(2,1)} %param.8) | copy-start | bytes 11010052
  77.4 2.6 %copy-start = (bf16[128,4,3584]{2,1,0:T(4,128)(2,1)}, bf16[128,4,3584]{2,1,0:T(4,128)(2,1)S(1)}, u32[]{:S(2)}) copy-start(bf16[128,4,3584]{2,1,0:T(4,128)(2,1)S(1)} %slice.19) | copy-start | bytes 11010052
  77.7 3.1 %copy-start.2 = (bf16[1,3584,512]{2,1,0:T(8,128)(2,1)S(1)}, bf16[1,3584,512]{2,1,0:T(8,128)(2,1)}, u32[]{:S(2)}) copy-start(bf16[1,3584,512]{2,1,0:T(8,128)(2,1)} %param.9) | copy-start | bytes 11010052
  92.0 52.6 %all-to-all-start.1 = ((bf16[128,4,3584]{2,1,0:T(4,128)(2,1)}), bf16[128,4,3584]{2,1,0:T(4,128)(2,1)}, u32[]{:S(2)}, u32[]{:S(2)}) async-start(bf16[128,4,3584]{2,1,0:T(4,128)(2,1)} %copy.28), calls=%async_computation.1 | async-start | bytes 7340032 | tf_op jit(solution)/shard_map/all_to_all | solution.py:69
  97.7 6.2 %copy-start.1 = (bf16[128,4,3584]{2,1,0:T(4,128)(2,1)S(1)}, bf16[128,4,3584]{2,1,0:T(4,128)(2,1)}, u32[]{:S(2)}) copy-start(bf16[128,4,3584]{2,1,0:T(4,128)(2,1)} %copy-done) | copy-start | bytes 11010052

commit v10 on v6

--- a/solution.py
+++ b/solution.py
@@ -64,9 +64,9 @@
     back, grad_g, grad_u = expert_math(got_rows, got_cot, w_gate[0], w_up[0])
 
     returned = lax.all_to_all(back, ("expert", "dp"), split_axis=0, concat_axis=0, tiled=True)
-    pick_dup = jnp.broadcast_to(
-        pick.reshape(n_experts, 1, most_rows, tok_rows), (n_experts, n_dp, most_rows, tok_rows)
-    ).reshape(n_experts * n_dp, most_rows, tok_rows)
+    source = jnp.arange(n_experts * n_dp, dtype=jnp.int32)[:, None, None]
+    slot = jnp.arange(most_rows, dtype=jnp.int32)[None, :, None]
+    pick_dup = ((source // n_dp) * most_rows + slot == dest[None, None, :]).astype(jnp.bfloat16)
     grad_tokens = lax.dot_general(
         pick_dup, returned, (((0, 1), (0, 1)), ((), ())), preferred_element_type=jnp.float32
     ).astype(jnp.bfloat16)

time: 148 us -> 149 us (level)
    broadcast_in_dim x2, local copies, waits for them, and re-layouts: 2.4 us -> 3.9 us  [per_device(): jnp.broadcast_to(send_rows, (n_experts, n_dp, most_rows, model_width))]
where the time goes in v10:
time: 149 us
  blocking collectives  64 us (43%)
  waiting for transfers between devices  36.8 us (25%)
  matrix products  24.6 us (17%)
  local copies, waits for them, and re-layouts  12.6 us (8%)
  starting transfers between devices  5.63 us (4%)
  other arithmetic  4.19 us (3%)
    all_to_all x1, blocking collectives, per_device(): lax.all_to_all(packed, ('expert', 'dp'), split_axis=0, concat_axis=0, til...  64 us
    all_to_all x1, waiting for transfers between devices, per_device(): lax.all_to_all(back, ('expert', 'dp'), split_axis=0, concat_axis=0, tiled...  36.8 us
    dot_general x1, matrix products, expert_math(): jnp.einsum('skd,skf->df', rows, d_gate, preferred_element_type=jnp.float32)  6.14 us
    all_to_all x1, starting transfers between devices, per_device(): lax.all_to_all(back, ('expert', 'dp'), split_axis=0, concat_axis=0, tiled...  5.63 us
    convert_element_type x1, local copies, waits for them, and re-layouts, expert_math(): back.astype(jnp.bfloat16)  4.67 us
    dot_general x1, matrix products, expert_math(): jnp.einsum('skf,df->skd', jnp.concatenate([d_gate, d_up], axis=2), jnp.co...  4.26 us
    dot_general x1, matrix products, expert_math(): jnp.einsum('skd,skf->df', rows, d_up, preferred_element_type=jnp.float32)  3.95 us
    broadcast_in_dim x2, local copies, waits for them, and re-layouts, per_device(): jnp.broadcast_to(send_rows, (n_experts, n_dp, most_rows, model_width))  3.9 us
  transfers between devices with their start and end apart: 1, of which 1 were waited for; matrix products, arithmetic and copies ran while one was open for 7% of the time, Pallas kernels for 0%

profile of v10, /device:TPU:1, one launch (start us, length us, event | category | flops | bytes accessed | tf_op | source)
XLA Modules:
  0.0 148.7 jit_solution(13694979769870403902)
XLA Ops:
  0.6 0.0 copy-start
  0.6 0.9 convert_reduce_fusion
  1.6 0.7 multiply_add_fusion
  2.2 1.2 convolution_convert_fusion.1
  3.5 0.4 reshape.91
  3.9 0.2 copy.18
  4.1 0.0 copy-done
  4.1 0.6 convolution_convert_fusion
  4.7 1.5 broadcast_in_dim.8
  6.2 2.4 %broadcast_in_dim.9 = bf16[64,2,4,3584]{3,2,1,0:T(4,128)(2,1)S(1)} broadcast(bf16[64,4,3584]{2,1,0:T(4,128)(2,1)} %broadcast_in_dim.8), dimensions={0,2,3} | broadcast | bytes 5505024 | tf_op jit(solution)/shard_map/broadcast_in_dim | solution.py:54
  8.6 2.6 %pad_maximum_fusion = bf16[64,2,4,4096]{3,2,1,0:T(4,128)(2,1)S(1)} fusion(bf16[64,2,4,512]{3,2,1,0:T(4,128)(2,1)S(1)} %copy.18, bf16[64,2,4,3584]{3,2,1,0:T(4,128)(2,1)S(1)} %broadcast_in_dim.9), kind=kLoop, calls=%fused_computation.12 | loop fusion | flops 8388608 | bytes 8388608 | tf_op jit(solution)/shard_map/concatenate | solution.py:52
  11.2 64.0 %all_to_all.10 = bf16[128,4,4096]{2,1,0:T(4,128)(2,1)S(1)} all-to-all(bf16[128,4,4096]{2,1,0:T(4,128)(2,1)S(1)} %bitcast.47), channel_id=1, replica_groups=mesh['expert'=64,'dp'=2] {'expert','dp'}, dimensions={0} | all-to-all | bytes 8388608 | tf_op jit(solution)/shard_map/all_to_all | solution.py:60
  75.2 0.3 slice.8
  75.5 0.0 copy-start.4
  75.5 1.8 %slice.9 = bf16[128,4,3584]{2,1,0:T(4,128)(2,1)S(1)} slice(bf16[128,4,4096]{2,1,0:T(4,128)(2,1)S(1)} %all_to_all.10), slice={[0:128], [0:4], [0:3584]} | slice | bytes 7340032 | tf_op jit(solution)/shard_map/slice | solution.py:61
  77.3 0.2 copy-done.4
  77.5 0.0 copy-start.1
  77.5 0.0 copy-start.3
  77.5 2.2 %fusion.37 = (bf16[128,4,512]{2,0,1:T(8,128)(2,1)S(1)}, f32[128,4,512]{2,0,1:T(8,128)S(1)}) fusion(bf16[128,4,512]{2,1,0:T(4,128)(2,1)S(1)} %slice.8, bf16[1,3584,512]{2,1,0:T(8,128)(2,1)S(1)} %copy-done.4, bf16[128,4,3584]{2,1,0:T(4,128)(2,1)S(1)} %slice.9), kind=kOutput, calls=%fused_computation.29 | convolution fusion | flops 1880883200 | bytes 9437184 | tf_op jit(solution)/shard_map/skd,df->skf/dot_general | solution.py:8
  79.8 0.0 copy-done.1
  79.8 1.1 copy-done.3
  80.9 2.3 %fusion.31 = bf16[128,4,512]{2,0,1:T(8,128)(2,1)S(1)} fusion(bf16[1,3584,512]{2,1,0:T(8,128)(2,1)S(1)} %copy-done.3, bf16[128,4,3584]{2,1,0:T(4,128)(2,1)S(1)} %slice.9, f32[128,4,512]{2,0,1:T(8,128)S(1)} %get-tuple-element.4, bf16[128,4,512]{2,1,0:T(4,128)(2,1)S(1)} %slice.8), kind=kOutput, calls=%fused_computation.26 | convolution fusion | flops 1881931776 | bytes 9437184 | tf_op jit(solution)/shard_map/skd,df->skf/dot_general | solution.py:9
  83.2 4.3 %fusion.3 = bf16[128,4,3584]{2,0,1:T(8,128)(2,1)S(1)} fusion(bf16[3584,512]{1,0:T(8,128)(2,1)S(1)} %bitcast.49, bf16[3584,512]{1,0:T(8,128)(2,1)S(1)} %bitcast.50, bf16[128,4,512]{2,0,1:T(8,128)(2,1)S(1)} %get-tuple-element.3, bf16[128,4,512]{2,0,1:T(8,128)(2,1)S(1)} %fusion.31), kind=kOutput, calls=%fused_computation.6 | convolution fusion | flops 3776708608 | bytes 12058624 | tf_op jit(solution)/shard_map/skf,df->skd/dot_general | solution.py:16
  87.5 4.7 %copy.21 = bf16[128,4,3584]{2,1,0:T(4,128)(2,1)} copy(bf16[128,4,3584]{2,0,1:T(8,128)(2,1)S(1)} %fusion.3) | data formatting | bytes 7340032 | tf_op jit(solution)/shard_map/convert_element_type | solution.py:24
  92.2 5.6 %all-to-all-start.1 = ((bf16[128,4,3584]{2,1,0:T(4,128)(2,1)}), bf16[128,4,3584]{2,1,0:T(4,128)(2,1)}, u32[]{:S(2)}, u32[]{:S(2)}) async-start(bf16[128,4,3584]{2,1,0:T(4,128)(2,1)} %copy.21), calls=%async_computation.1 | async-start | bytes 7340032 | tf_op jit(solution)/shard_map/all_to_all | solution.py:66
  97.8 0.0 copy-start.2
  97.8 6.1 %fusion.4 = bf16[1,3584,512]{2,1,0:T(8,128)(2,1)} fusion(bf16[128,4,512]{2,0,1:T(8,128)(2,1)S(1)} %fusion.31, bf16[128,4,3584]{2,1,0:T(4,128)(2,1)} %copy-done.1), kind=kOutput, calls=%fused_computation.7 | convolution fusion | flops 1880883200 | bytes 7864320 | tf_op jit(solution)/shard_map/skd,skf->df/dot_general | solution.py:22
  104.0 0.0 copy-done.2
  104.0 4.0 %fusion.5 = bf16[1,3584,512]{2,1,0:T(8,128)(2,1)} fusion(bf16[128,4,512]{2,0,1:T(8,128)(2,1)S(1)} %get-tuple-element.3, bf16[128,4,3584]{2,1,0:T(4,128)(2,1)S(1)} %copy-done.2), kind=kOutput, calls=%fused_computation.8 | convolution fusion | flops 1880883200 | bytes 7864320 | tf_op jit(solution)/shard_map/skd,skf->df/dot_general | solution.py:23
  107.9 36.8 %all-to-all-done.1 = bf16[128,4,3584]{2,1,0:T(4,128)(2,1)} async-done(((bf16[128,4,3584]{2,1,0:T(4,128)(2,1)}), bf16[128,4,3584]{2,1,0:T(4,128)(2,1)}, u32[]{:S(2)}, u32[]{:S(2)}) %all-to-all-start.1) | async-done | bytes 3670048 | tf_op jit(solution)/shard_map/all_to_all | solution.py:66
  144.8 3.9 %fusion.6 = bf16[128,3584]{1,0:T(8,128)(2,1)} fusion(bf16[128,4,3584]{2,1,0:T(4,128)(2,1)} %all-to-all-done.1, s32[128,4]{0,1:T(4,128)S(1)} %iota_add_fusion, s32[128]{0:T(128)S(1)} %multiply_add_fusion), kind=kOutput, calls=%fused_computation.11 | convolution fusion | flops 470286336 | bytes 4590080 | tf_op jit(solution)/shard_map/dot_general | solution.py:70
  (2 shorter events, 0.0 us)
Async XLA Ops:
  0.6 3.4 %copy-start = (bf16[128,3584]{1,0:T(8,128)(2,1)S(1)}, bf16[128,3584]{1,0:T(8,128)(2,1)}, u32[]{:S(2)}) copy-start(bf16[128,3584]{1,0:T(8,128)(2,1)} %param.5) | copy-start | bytes 2752516
  75.5 2.0 %copy-start.4 = (bf16[1,3584,512]{2,1,0:T(8,128)(2,1)S(1)}, bf16[1,3584,512]{2,1,0:T(8,128)(2,1)}, u32[]{:S(2)}) copy-start(bf16[1,3584,512]{2,1,0:T(8,128)(2,1)} %param.8) | copy-start | bytes 11010052
  77.5 2.2 %copy-start.1 = (bf16[128,4,3584]{2,1,0:T(4,128)(2,1)}, bf16[128,4,3584]{2,1,0:T(4,128)(2,1)S(1)}, u32[]{:S(2)}) copy-start(bf16[128,4,3584]{2,1,0:T(4,128)(2,1)S(1)} %slice.9) | copy-start | bytes 11010052
  77.5 3.4 %copy-start.3 = (bf16[1,3584,512]{2,1,0:T(8,128)(2,1)S(1)}, bf16[1,3584,512]{2,1,0:T(8,128)(2,1)}, u32[]{:S(2)}) copy-start(bf16[1,3584,512]{2,1,0:T(8,128)(2,1)} %param.9) | copy-start | bytes 11010052
  92.2 52.6 %all-to-all-start.1 = ((bf16[128,4,3584]{2,1,0:T(4,128)(2,1)}), bf16[128,4,3584]{2,1,0:T(4,128)(2,1)}, u32[]{:S(2)}, u32[]{:S(2)}) async-start(bf16[128,4,3584]{2,1,0:T(4,128)(2,1)} %copy.21), calls=%async_computation.1 | async-start | bytes 7340032 | tf_op jit(solution)/shard_map/all_to_all | solution.py:66
  97.8 6.2 %copy-start.2 = (bf16[128,4,3584]{2,1,0:T(4,128)(2,1)S(1)}, bf16[128,4,3584]{2,1,0:T(4,128)(2,1)}, u32[]{:S(2)}) copy-start(bf16[128,4,3584]{2,1,0:T(4,128)(2,1)} %copy-done.1) | copy-start | bytes 11010052

commit v11 on v5

--- a/solution.py
+++ b/solution.py
@@ -41,10 +41,11 @@
     slot_total = n_experts * most_rows
 
     expert_of = routing[:, 0]
-    one_hot = (expert_of[:, None] == jnp.arange(n_experts, dtype=jnp.int32)[None, :]).astype(
-        jnp.int32
-    )
-    slot_of = jnp.sum(jnp.cumsum(one_hot, axis=0) * one_hot, axis=1) - 1
+    same = expert_of[:, None] == expert_of[None, :]
+    earlier = jnp.arange(tok_rows, dtype=jnp.int32)[None, :] < jnp.arange(
+        tok_rows, dtype=jnp.int32
+    )[:, None]
+    slot_of = jnp.sum((same & earlier).astype(jnp.int32), axis=1)
     dest = expert_of * most_rows + slot_of
     pick = (jnp.arange(slot_total, dtype=jnp.int32)[:, None] == dest[None, :]).astype(
         jnp.bfloat16

time: 150 us -> 149 us (level)
  no operation moved by 1% of the time
where the time goes in v11:
time: 149 us
  blocking collectives  64 us (43%)
  waiting for transfers between devices  36.8 us (25%)
  matrix products  23.9 us (16%)
  local copies, waits for them, and re-layouts  13 us (9%)
  starting transfers between devices  5.61 us (4%)
  other arithmetic  4.85 us (3%)
    all_to_all x1, blocking collectives, per_device(): lax.all_to_all(packed, ('expert', 'dp'), split_axis=0, concat_axis=0, til...  64 us
    all_to_all x1, waiting for transfers between devices, per_device(): lax.all_to_all(back, ('expert', 'dp'), split_axis=0, concat_axis=0, tiled...  36.8 us
    dot_general x1, matrix products, expert_math(): jnp.einsum('skd,skf->df', rows, d_up, preferred_element_type=jnp.float32)  6.14 us
    all_to_all x1, starting transfers between devices, per_device(): lax.all_to_all(back, ('expert', 'dp'), split_axis=0, concat_axis=0, tiled...  5.61 us
    convert_element_type x1, local copies, waits for them, and re-layouts, expert_math(): back.astype(jnp.bfloat16)  4.66 us
    dot_general x1, matrix products, expert_math(): jnp.einsum('skf,df->skd', jnp.concatenate([d_gate, d_up], axis=2), jnp.co...  4.25 us
    dot_general x1, matrix products, expert_math(): jnp.einsum('skd,df->skf', rows, jnp.concatenate([weight_gate, weight_up],...  3.98 us
    dot_general x1, matrix products, expert_math(): jnp.einsum('skd,skf->df', rows, d_gate, preferred_element_type=jnp.float32)  3.95 us
  transfers between devices with their start and end apart: 1, of which 1 were waited for; matrix products, arithmetic and copies ran while one was open for 7% of the time, Pallas kernels for 0%

profile of v11, /device:TPU:1, one launch (start us, length us, event | category | flops | bytes accessed | tf_op | source)
XLA Modules:
  0.0 148.9 jit_solution(1714089409502748264)
XLA Ops:
  0.6 0.0 copy-start
  0.6 0.0 copy-start.4
  0.7 0.9 convert_reduce_fusion
  1.6 0.7 multiply_add_fusion.1
  2.3 0.0 copy-done
  2.3 0.6 convolution_convert_fusion.1
  2.9 1.5 broadcast_in_dim.11
  4.3 0.0 copy-done.4
  4.3 0.0 copy-start.1
  4.3 1.1 convolution_convert_fusion.2
  5.4 1.4 reshape.43
  6.9 0.2 copy.25
  7.1 0.0 copy-done.1
  7.1 0.9 broadcast_in_dim.24
  8.0 2.6 %pad_maximum_fusion = bf16[64,2,4,4096]{3,2,1,0:T(4,128)(2,1)S(1)} fusion(bf16[64,2,4,512]{3,2,1,0:T(4,128)(2,1)S(1)} %copy.25, bf16[64,2,4,3584]{3,2,1,0:T(4,128)(2,1)S(1)} %broadcast_in_dim.24), kind=kLoop, calls=%fused_computation.10 | loop fusion | flops 8388608 | bytes 8388608 | tf_op jit(solution)/shard_map/concatenate | solution.py:59
  10.7 64.0 %all_to_all.10 = bf16[128,4,4096]{2,1,0:T(4,128)(2,1)S(1)} all-to-all(bf16[128,4,4096]{2,1,0:T(4,128)(2,1)S(1)} %bitcast.32), channel_id=1, replica_groups=mesh['expert'=64,'dp'=2] {'expert','dp'}, dimensions={0} | all-to-all | bytes 8388608 | tf_op jit(solution)/shard_map/all_to_all | solution.py:67
  74.7 0.0 copy-start.5
  74.7 0.0 copy-start.6
  74.7 1.8 %slice.17 = bf16[128,4,3584]{2,1,0:T(4,128)(2,1)S(1)} slice(bf16[128,4,4096]{2,1,0:T(4,128)(2,1)S(1)} %all_to_all.10), slice={[0:128], [0:4], [0:3584]} | slice | bytes 7340032 | tf_op jit(solution)/shard_map/slice | solution.py:68
  76.5 0.0 copy-start.2
  76.5 0.2 copy-done.5
  76.7 1.9 %copy-done.6 = bf16[1,3584,512]{2,1,0:T(8,128)(2,1)S(1)} copy-done((bf16[1,3584,512]{2,1,0:T(8,128)(2,1)S(1)}, bf16[1,3584,512]{2,1,0:T(8,128)(2,1)}, u32[]{:S(2)}) %copy-start.6) | copy-done | bytes 3670040
  78.6 4.0 %fusion.3 = f32[128,4,1024]{2,0,1:T(8,128)S(1)} fusion(bf16[3584,512]{1,0:T(8,128)(2,1)S(1)} %bitcast.35, bf16[3584,512]{1,0:T(8,128)(2,1)S(1)} %bitcast.37, bf16[128,4,3584]{2,1,0:T(4,128)(2,1)S(1)} %slice.17), kind=kOutput, calls=%fused_computation.9 | convolution fusion | flops 3772776448 | bytes 13107200 | tf_op jit(solution)/shard_map/skd,df->skf/dot_general | solution.py:9
  82.6 0.0 copy-done.2
  82.6 0.3 slice.16
  82.9 0.5 fusion.10
  83.4 4.3 %convolution_convert_fusion = bf16[128,4,3584]{2,0,1:T(8,128)(2,1)S(1)} fusion(bf16[3584,512]{1,0:T(8,128)(2,1)S(1)} %bitcast.36, bf16[3584,512]{1,0:T(8,128)(2,1)S(1)} %bitcast.38, bf16[128,4,512]{2,0,1:T(8,128)(2,1)S(1)} %get-tuple-element.4, bf16[128,4,512]{2,0,1:T(8,128)(2,1)S(1)} %get-tuple-element.3), kind=kOutput, calls=%fused_computation.3 | convolution fusion | flops 3776708608 | bytes 12058624 | tf_op jit(solution)/shard_map/skf,df->skd/dot_general | solution.py:23
  87.7 4.7 %copy.28 = bf16[128,4,3584]{2,1,0:T(4,128)(2,1)} copy(bf16[128,4,3584]{2,0,1:T(8,128)(2,1)S(1)} %convolution_convert_fusion) | data formatting | bytes 7340032 | tf_op jit(solution)/shard_map/convert_element_type | solution.py:31
  92.3 5.6 %all-to-all-start.1 = ((bf16[128,4,3584]{2,1,0:T(4,128)(2,1)}), bf16[128,4,3584]{2,1,0:T(4,128)(2,1)}, u32[]{:S(2)}, u32[]{:S(2)}) async-start(bf16[128,4,3584]{2,1,0:T(4,128)(2,1)} %copy.28), calls=%async_computation.1 | async-start | bytes 7340032 | tf_op jit(solution)/shard_map/all_to_all | solution.py:73
  98.0 0.1 compare_convert_fusion
  98.1 0.0 copy-start.3
  98.1 6.1 %fusion.1 = bf16[1,3584,512]{2,1,0:T(8,128)(2,1)} fusion(bf16[128,4,512]{2,0,1:T(8,128)(2,1)S(1)} %get-tuple-element.4, bf16[128,4,3584]{2,1,0:T(4,128)(2,1)} %copy-done.2), kind=kOutput, calls=%fused_computation.5 | convolution fusion | flops 1880883200 | bytes 7864320 | tf_op jit(solution)/shard_map/skd,skf->df/dot_general | solution.py:30
  104.2 0.0 copy-done.3
  104.2 3.9 %fusion = bf16[1,3584,512]{2,1,0:T(8,128)(2,1)} fusion(bf16[128,4,512]{2,0,1:T(8,128)(2,1)S(1)} %get-tuple-element.3, bf16[128,4,3584]{2,1,0:T(4,128)(2,1)S(1)} %copy-done.3), kind=kOutput, calls=%fused_computation.4 | convolution fusion | flops 1880883200 | bytes 7864320 | tf_op jit(solution)/shard_map/skd,skf->df/dot_general | solution.py:29
  108.2 36.8 %all-to-all-done.1 = bf16[128,4,3584]{2,1,0:T(4,128)(2,1)} async-done(((bf16[128,4,3584]{2,1,0:T(4,128)(2,1)}), bf16[128,4,3584]{2,1,0:T(4,128)(2,1)}, u32[]{:S(2)}, u32[]{:S(2)}) %all-to-all-start.1) | async-done | bytes 3670048 | tf_op jit(solution)/shard_map/all_to_all | solution.py:73
  144.9 0.1 broadcast_in_dim.10
  145.0 3.9 %fusion.2 = bf16[128,3584]{1,0:T(8,128)(2,1)} fusion(bf16[128,4,128]{2,0,1:T(8,128)(2,1)S(1)} %bitcast.34, bf16[128,4,3584]{2,1,0:T(4,128)(2,1)} %all-to-all-done.1), kind=kOutput, calls=%fused_computation.8 | convolution fusion | flops 470220800 | bytes 4718592 | tf_op jit(solution)/shard_map/dot_general | solution.py:77
  (1 shorter events, 0.0 us)
Async XLA Ops:
  0.6 1.6 %copy-start = (bf16[128,3584]{1,0:T(8,128)(2,1)S(1)}, bf16[128,3584]{1,0:T(8,128)(2,1)}, u32[]{:S(2)}) copy-start(bf16[128,3584]{1,0:T(8,128)(2,1)} %param.5) | copy-start | bytes 2752516
  0.6 3.7 %copy-start.4 = (bf16[128,1024]{1,0:T(8,128)(2,1)S(1)}, bf16[128,1024]{1,0:T(8,128)(2,1)}, u32[]{:S(2)}) copy-start(bf16[128,1024]{1,0:T(8,128)(2,1)} %param.6) | copy-start | bytes 786436
  4.3 2.7 %copy-start.1 = (bf16[64,4,3584]{2,1,0:T(4,128)(2,1)S(1)}, bf16[64,4,3584]{2,1,0:T(4,128)(2,1)}, u32[]{:S(2)}) copy-start(bf16[64,4,3584]{2,1,0:T(4,128)(2,1)} %broadcast_in_dim.11) | copy-start | bytes 5505028
  74.7 2.0 %copy-start.5 = (bf16[1,3584,512]{2,1,0:T(8,128)(2,1)S(1)}, bf16[1,3584,512]{2,1,0:T(8,128)(2,1)}, u32[]{:S(2)}) copy-start(bf16[1,3584,512]{2,1,0:T(8,128)(2,1)} %param.9) | copy-start | bytes 11010052
  74.7 3.9 %copy-start.6 = (bf16[1,3584,512]{2,1,0:T(8,128)(2,1)S(1)}, bf16[1,3584,512]{2,1,0:T(8,128)(2,1)}, u32[]{:S(2)}) copy-start(bf16[1,3584,512]{2,1,0:T(8,128)(2,1)} %param.8) | copy-start | bytes 11010052
  76.5 6.1 %copy-start.2 = (bf16[128,4,3584]{2,1,0:T(4,128)(2,1)}, bf16[128,4,3584]{2,1,0:T(4,128)(2,1)S(1)}, u32[]{:S(2)}) copy-start(bf16[128,4,3584]{2,1,0:T(4,128)(2,1)S(1)} %slice.17) | copy-start | bytes 11010052
  92.3 52.6 %all-to-all-start.1 = ((bf16[128,4,3584]{2,1,0:T(4,128)(2,1)}), bf16[128,4,3584]{2,1,0:T(4,128)(2,1)}, u32[]{:S(2)}, u32[]{:S(2)}) async-start(bf16[128,4,3584]{2,1,0:T(4,128)(2,1)} %copy.28), calls=%async_computation.1 | async-start | bytes 7340032 | tf_op jit(solution)/shard_map/all_to_all | solution.py:73
  98.1 6.2 %copy-start.3 = (bf16[128,4,3584]{2,1,0:T(4,128)(2,1)S(1)}, bf16[128,4,3584]{2,1,0:T(4,128)(2,1)}, u32[]{:S(2)}) copy-start(bf16[128,4,3584]{2,1,0:T(4,128)(2,1)} %copy-done.2) | copy-start | bytes 11010052
